TPU v7x, 128 devices: a whole 4x4x4 slice. The times are simulated.
128 devices in a mesh: req: 8 (over x, core), mlp: 16 (over y, z).
Axes of the slice: x: 4, y: 4, z: 4, core: 2. Of those that a mesh axis runs over, the one named last changes fastest.
Arguments:
- hidden_in: bfloat16 [16384, 2560], P(('req', 'mlp')), may hold values from -6 to 6
- queries: bfloat16 [16384, 2048], P(('req', 'mlp')), may hold values from -120 to 120
- keys_new: bfloat16 [16384, 512], P(('req', 'mlp')), may hold values from -4.4 to 4.4
- values_new: bfloat16 [16384, 512], P(('req', 'mlp')), may hold values from -5 to 5
- keys_cache: bfloat16 [4096, 512], P('req'), may hold values from -4.4 to 4.4
- values_cache: bfloat16 [4096, 512], P('req'), may hold values from -5 to 5
- out_weight: bfloat16 [2048, 2560], replicated, may hold values from -0.375 to 0.375
- norm_gain: float32 [2560], replicated, may hold values from 0.25 to 1.75
- gate_weight: bfloat16 [2560, 9728], P(None, 'mlp'), may hold values from -0.125 to 0.125
- up_weight: bfloat16 [2560, 9728], P(None, 'mlp'), may hold values from -0.125 to 0.125
- down_weight: bfloat16 [9728, 2560], P('mlp'), may hold values from -0.0625 to 0.0625
- lengths: int32 [8, 16], P('req', 'mlp'), may hold values from 1 to 128, 1536 in all within a row
- slot_request: int32 [128], replicated, may hold values from 0 to 127, each once
- cache_group: int32 [8, 4], replicated, may hold values from 0 to 3, each once within a row
Outputs:
- output: bfloat16 [16384, 2560], P(('req', 'mlp'))
Inputs may be any that keep to these rules, and one draw needn't show every extreme that they name: The 16 entries of one row of lengths sum to 1536, and one of them is 128. `slot_request`: each request appears in one slot. `cache_group`: each row names every group once.
All inputs are finite; a program needn't handle non-finite values. No bound on the sum of `lengths` on one device may be relied on, other than what follows from the above.
Results may differ from a plain program's by a relative error of at most 0.014.
Values may be sent and summed in bfloat16 or wider, within the bound.
No kernel may reach another device: no remote copies, remote signals or barrier semaphores. Data moves between devices by JAX's collectives and lax.ppermute only.
A program may use at most 128 MiB of HBM per device.

v0:
```python
import jax
import jax.numpy as jnp
from jax import lax
from jax.sharding import PartitionSpec as P

HEADS = 16
KVH = 4
HD = 128
GROUPS = 4


NEGATIVE = -1e30
EPSILON = 1e-06


def partial_attention(query_block, key_rows, value_rows, allowed):
    row_count = query_block.shape[0]
    key_count = key_rows.shape[0]
    per_group = HEADS // KVH
    query_heads = query_block.reshape(row_count, KVH, per_group, HD)
    key_heads = key_rows.reshape(key_count, KVH, HD)
    value_heads = value_rows.reshape(key_count, KVH, HD)
    scores = jnp.einsum(
        "tkgd,skd->kgts", query_heads, key_heads, preferred_element_type=jnp.float32
    ) * HD ** (-0.5)
    if allowed is not None:
        scores = jnp.where(allowed, scores, NEGATIVE)
    maxima = jnp.max(scores, axis=3)
    weights = jnp.exp(scores - maxima[..., None])
    totals = jnp.sum(weights, axis=3)
    context = jnp.einsum(
        "kgts,skd->tkgd",
        weights.astype(jnp.bfloat16),
        value_heads,
        preferred_element_type=jnp.float32,
    )
    context = context.reshape(row_count, HEADS * HD)
    maxima = jnp.transpose(maxima, (2, 0, 1)).reshape(row_count, HEADS)
    totals = jnp.transpose(totals, (2, 0, 1)).reshape(row_count, HEADS)
    return (context, maxima, totals)


def merge_pair(earlier, latest):
    context_early, maxima_early, totals_early = earlier
    context_late, maxima_late, totals_late = latest
    row_count = context_early.shape[0]
    highest = jnp.maximum(maxima_early, maxima_late)
    factor_early = jnp.exp(maxima_early - highest)
    factor_late = jnp.exp(maxima_late - highest)
    context = (
        context_early.reshape(row_count, HEADS, HD) * factor_early[..., None]
        + context_late.reshape(row_count, HEADS, HD) * factor_late[..., None]
    )
    return (
        context.reshape(row_count, HEADS * HD),
        highest,
        totals_early * factor_early + totals_late * factor_late,
    )


def shards(
    hidden_in,
    queries,
    keys_new,
    values_new,
    keys_cache,
    values_cache,
    out_weight,
    norm_gain,
    gate_weight,
    up_weight,
    down_weight,
    lengths,
    slot_request,
    cache_group,
):
    owners = lax.axis_size("req")
    columns = lax.axis_size("mlp")
    owner_index = lax.axis_index("req")
    column_index = lax.axis_index("mlp")
    tokens = queries.shape[0]
    width_kv = keys_cache.shape[1]
    piece_rows = keys_cache.shape[0] // GROUPS
    slot_group = slot_request // (slot_request.shape[0] // GROUPS)
    own_row = cache_group[owner_index]
    wanted = lax.dynamic_slice_in_dim(slot_group.reshape(owners, columns), column_index, 1, 1)[:, 0]
    group_ids = jnp.arange(GROUPS, dtype=jnp.int32)
    sub_block = jnp.sum(
        jnp.where(own_row[None, :] == wanted[:, None], group_ids[None, :], 0), axis=1
    )
    slab_keys = keys_cache.reshape(GROUPS, piece_rows, width_kv)
    slab_values = values_cache.reshape(GROUPS, piece_rows, width_kv)
    positions = jnp.arange(tokens, dtype=jnp.int32)
    causal = positions[:, None] >= positions[None, :]
    local_part = partial_attention(queries, keys_new, values_new, causal)
    send_keys = jnp.take(slab_keys, sub_block, axis=0)
    send_values = jnp.take(slab_values, sub_block, axis=0)
    got_keys, got_values = (
        lax.all_to_all(send_keys, "req", split_axis=0, concat_axis=0, tiled=True),
        lax.all_to_all(send_values, "req", split_axis=0, concat_axis=0, tiled=True),
    )
    prefix_part = partial_attention(
        queries,
        got_keys.reshape(owners * piece_rows, width_kv),
        got_values.reshape(owners * piece_rows, width_kv),
        None,
    )
    context, highest, totals = merge_pair(local_part, prefix_part)
    context = context.reshape(tokens, HEADS, HD)
    context = (context / totals[..., None]).reshape(tokens, HEADS * HD).astype(jnp.bfloat16)
    attended = jnp.dot(context, out_weight, preferred_element_type=jnp.float32)
    residual = (hidden_in.astype(jnp.float32) + attended).astype(jnp.bfloat16)
    widened = residual.astype(jnp.float32)
    normed = (
        widened
        * lax.rsqrt(jnp.mean(widened * widened, axis=1, keepdims=True) + EPSILON)
        * norm_gain[None, :]
    ).astype(jnp.bfloat16)
    shard_rows = lax.all_gather(normed, "mlp", axis=0, tiled=True)
    gate_values = jnp.dot(shard_rows, gate_weight, preferred_element_type=jnp.float32)
    upward = jnp.dot(shard_rows, up_weight, preferred_element_type=jnp.float32)
    hidden = (jax.nn.silu(gate_values) * upward).astype(jnp.bfloat16)
    partial_terms = jnp.dot(hidden, down_weight, preferred_element_type=jnp.float32)
    mixed = lax.psum_scatter(
        partial_terms.astype(jnp.bfloat16), "mlp", scatter_dimension=0, tiled=True
    ).astype(jnp.float32)
    result = residual.astype(jnp.float32) + mixed
    live_slot = positions[:, None] < lengths[0, 0]
    return jnp.where(live_slot, result, 0.0).astype(jnp.bfloat16)


def solution(mesh):
    return jax.shard_map(
        shards,
        mesh=mesh,
        in_specs=(
            P(("req", "mlp"), None),
            P(("req", "mlp"), None),
            P(("req", "mlp"), None),
            P(("req", "mlp"), None),
            P("req", None),
            P("req", None),
            P(),
            P(),
            P(None, "mlp"),
            P(None, "mlp"),
            P("mlp", None),
            P("req", "mlp"),
            P(),
            P(),
        ),
        out_specs=P(("req", "mlp"), None),
        check_vma=False,
    )
```

profile of v0, /device:TPU:0, one launch (start us, length us, event | category | flops | bytes accessed | tf_op | source)
XLA Modules:
  0.0 287.3 jit_solution(5620928909980571331)
XLA Ops:
  6.5 0.0 copy-start
  6.5 0.8 and_select_fusion
  7.4 0.1 reshape.109
  7.4 0.2 dynamic-slice_reduce_fusion
  7.6 0.9 dynamic-slice_reduce_fusion.1
  8.5 0.1 select_reduce_fusion
  8.6 2.6 gather_fusion
  11.2 0.0 copy-start.6
  11.2 0.0 copy-start.7
  11.2 2.7 gather_fusion.1
  13.9 3.1 %broadcast_select_fusion = (bf16[8,128,512]{2,1,0:T(8,128)(2,1)}, bf16[8,128,512]{2,1,0:T(8,128)(2,1)}) fusion(bf16[8,128,512]{2,1,0:T(8,128)(2,1)} %gather_fusion.1, pred[8]{0:T(512)(128)(4,1)S(1)} %compare_and_fusion, bf16[8,128,512]{2,1,0:T(8,128)(2,1)} %gather_fusion), kind=kLoop, calls=%fused_computation.31 | loop fusion | flops 1048576 | bytes 4194312 | tf_op jit(solution)/shard_map/jit(_take)/select_n | solution.py:97
  17.0 4.4 %all-to-all-start = ((bf16[8,128,512]{2,1,0:T(8,128)(2,1)}), bf16[8,128,512]{2,1,0:T(8,128)(2,1)}, u32[]{:S(2)}, u32[]{:S(2)}) async-start(bf16[8,128,512]{2,1,0:T(8,128)(2,1)} %get-tuple-element.10), calls=%async_computation | async-start | bytes 2097152 | tf_op jit(solution)/shard_map/all_to_all | solution.py:99
  21.4 2.2 reshape.105
  23.6 0.0 copy-done.6
  23.7 0.0 copy-done.7
  23.7 0.1 copy.55
  23.8 1.4 fusion.32
  25.2 0.2 fusion.18
  25.4 1.4 fusion.20
  26.8 10.7 %all-to-all-done = bf16[8,128,512]{2,1,0:T(8,128)(2,1)} async-done(((bf16[8,128,512]{2,1,0:T(8,128)(2,1)}), bf16[8,128,512]{2,1,0:T(8,128)(2,1)}, u32[]{:S(2)}, u32[]{:S(2)}) %all-to-all-start) | async-done | bytes 1048608 | tf_op jit(solution)/shard_map/all_to_all | solution.py:99
  37.5 4.2 %all-to-all-start.1 = ((bf16[8,128,512]{2,1,0:T(8,128)(2,1)}), bf16[8,128,512]{2,1,0:T(8,128)(2,1)}, u32[]{:S(2)}, u32[]{:S(2)}) async-start(bf16[8,128,512]{2,1,0:T(8,128)(2,1)} %get-tuple-element.9), calls=%async_computation.1 | async-start | bytes 2097152 | tf_op jit(solution)/shard_map/all_to_all | solution.py:100
  41.7 0.0 all-gather.2.cloned.1.call-start
  41.8 2.2 reshape.140
  44.0 2.6 bitcast_reduce_fusion
  46.6 0.0 copy-start.2
  46.6 3.2 %copy-done.2 = f32[4,1024,128,4]{2,1,3,0:T(8,128)} copy-done((f32[4,1024,128,4]{2,1,3,0:T(8,128)}, f32[4,1024,128,4]{2,1,3,0:T(8,128)S(1)}, u32[]{:S(2)}) %copy-start.2) | copy-done | bytes 8388632
  49.8 1.4 fusion.1
  51.3 6.4 %all-to-all-done.1 = bf16[8,128,512]{2,1,0:T(8,128)(2,1)} async-done(((bf16[8,128,512]{2,1,0:T(8,128)(2,1)}), bf16[8,128,512]{2,1,0:T(8,128)(2,1)}, u32[]{:S(2)}, u32[]{:S(2)}) %all-to-all-start.1) | async-done | bytes 1048608 | tf_op jit(solution)/shard_map/all_to_all | solution.py:100
  57.7 2.1 reshape.141
  59.8 5.4 %fusion.3 = f32[4,128,4,128]{3,1,2,0:T(8,128)S(1)} fusion(f32[4,1024,128,4]{2,1,3,0:T(8,128)} %copy-done.2, f32[4,4,128]{2,1,0:T(4,128)S(1)} %get-tuple-element.11, bf16[1024,4,128,1]{2,1,0,3:T(4,128)(2,1)} %bitcast.68), kind=kOutput, calls=%fused_computation.9 | convolution fusion | flops 543162368 | bytes 10493952 | tf_op jit(solution)/shard_map/kgts,skd->tkgd/dot_general | solution.py:31
  65.2 0.0 copy-done.4
  65.2 0.2 fusion.14
  65.4 0.0 copy-done.5
  65.4 0.0 copy-start.8
  65.5 5.6 %multiply_reduce_fusion = (f32[128]{0:T(128)S(1)}, f32[128,2560]{1,0:T(8,128)S(1)}) fusion(bf16[128,2048]{0,1:T(8,128)(2,1)S(1)} %fusion.14, bf16[2048,2560]{1,0:T(8,128)(2,1)} %param.22, bf16[128,2560]{1,0:T(8,128)(2,1)S(1)} %copy-done.5), kind=kOutput, calls=%fused_computation.21 | convolution fusion | flops 1344143232 | bytes 12976640 | tf_op jit(solution)/shard_map/dot_general | solution.py:111
  71.1 1.1 copy-done.3
  72.2 0.0 copy-done.8
  72.2 1.0 multiply_convert_fusion.1
  73.2 0.0 all-gather.2.cloned.1.call-update
  73.2 0.2 reduce-scatter.2.cloned.1.call-start
  73.4 80.9 %all-gather.2.cloned.1.call-done = bf16[2048,2560]{1,0:T(8,128)(2,1)} async-done(((bf16[128,2560]{1,0:T(8,128)(2,1)}), bf16[2048,2560]{1,0:T(8,128)(2,1)}) %all-gather.2.cloned.1.call-update) | async-done | bytes 10485776 | tf_op jit(solution)/shard_map/all_gather | solution.py:119
  154.3 11.7 %fusion.33 = f32[2048,608]{0,1:T(8,128)} fusion(bf16[2048,2560]{1,0:T(8,128)(2,1)} %all-gather.2.cloned.1.call-done, bf16[2560,608]{0,1:T(8,128)(2,1)} %param.24), kind=kOutput, calls=%fused_computation.61 | convolution fusion | flops 6375342080 | bytes 18579456 | tf_op jit(solution)/shard_map/dot_general | solution.py:120
  166.1 0.0 copy-done
  166.1 21.7 %convolution_convert_fusion = bf16[2048,2560]{1,0:T(8,128)(2,1)} fusion(bf16[608,2560]{1,0:T(8,128)(2,1)S(1)} %copy-done, f32[2048,608]{0,1:T(8,128)} %fusion.33, bf16[2048,2560]{1,0:T(8,128)(2,1)} %all-gather.2.cloned.1.call-done, bf16[2560,608]{0,1:T(8,128)(2,1)} %param.25), kind=kOutput, calls=%fused_computation.2 | convolution fusion | flops 12763398144 | bytes 32178176 | tf_op jit(solution)/shard_map/dot_general | solution.py:123
  187.8 0.0 reduce-scatter.2.cloned.1.call-update
  188.6 89.3 %reduce-scatter.2.cloned.1.call-done = bf16[128,2560]{1,0:T(8,128)(2,1)} async-done(((bf16[2048,2560]{1,0:T(8,128)(2,1)}), bf16[128,2560]{1,0:T(8,128)(2,1)}) %reduce-scatter.2.cloned.1.call-update) | async-done | bytes 655376 | tf_op jit(solution)/shard_map/reduce_scatter | solution.py:124
  278.0 2.5 select_convert_fusion
  280.5 0.0 copy-done.1
  (12 shorter events, 0.1 us)
Async XLA Ops:
  6.5 159.5 %copy-start = (bf16[608,2560]{1,0:T(8,128)(2,1)S(1)}, bf16[608,2560]{1,0:T(8,128)(2,1)}, u32[]{:S(2)}) copy-start(bf16[608,2560]{1,0:T(8,128)(2,1)} %param.26) | copy-start | bytes 9338884
  11.2 12.4 %copy-start.6 = (bf16[128,512]{1,0:T(8,128)(2,1)S(1)}, bf16[128,512]{1,0:T(8,128)(2,1)}, u32[]{:S(2)}) copy-start(bf16[128,512]{1,0:T(8,128)(2,1)} %param.18) | copy-start | bytes 393220
  11.2 12.4 %copy-start.7 = (bf16[128,512]{1,0:T(8,128)(2,1)S(1)}, bf16[128,512]{1,0:T(8,128)(2,1)}, u32[]{:S(2)}) copy-start(bf16[128,512]{1,0:T(8,128)(2,1)} %param.19) | copy-start | bytes 393220
  17.0 20.5 %all-to-all-start = ((bf16[8,128,512]{2,1,0:T(8,128)(2,1)}), bf16[8,128,512]{2,1,0:T(8,128)(2,1)}, u32[]{:S(2)}, u32[]{:S(2)}) async-start(bf16[8,128,512]{2,1,0:T(8,128)(2,1)} %get-tuple-element.10), calls=%async_computation | async-start | bytes 2097152 | tf_op jit(solution)/shard_map/all_to_all | solution.py:99
  37.5 20.2 %all-to-all-start.1 = ((bf16[8,128,512]{2,1,0:T(8,128)(2,1)}), bf16[8,128,512]{2,1,0:T(8,128)(2,1)}, u32[]{:S(2)}, u32[]{:S(2)}) async-start(bf16[8,128,512]{2,1,0:T(8,128)(2,1)} %get-tuple-element.9), calls=%async_computation.1 | async-start | bytes 2097152 | tf_op jit(solution)/shard_map/all_to_all | solution.py:100
  41.7 112.6 %all-gather.2.cloned.1.call-start = ((), (), s32[]{:S(2)}) async-start(), calls=%async_computation.3 | async-start | bytes 11141120 | tf_op jit(solution)/shard_map/all_gather | solution.py:119
  46.6 3.2 %copy-start.2 = (f32[4,1024,128,4]{2,1,3,0:T(8,128)}, f32[4,1024,128,4]{2,1,3,0:T(8,128)S(1)}, u32[]{:S(2)}) copy-start(f32[4,1024,128,4]{2,1,3,0:T(8,128)S(1)} %get-tuple-element.12) | copy-start | bytes 25165828
  59.8 5.4 %copy-start.4 = (f32[4,4,128,128]{2,3,1,0:T(8,128)S(1)}, f32[4,4,128,128]{2,3,1,0:T(8,128)}, u32[]{:S(2)}) copy-start(f32[4,4,128,128]{2,3,1,0:T(8,128)} %fusion.20) | copy-start | bytes 3145732
  59.8 5.6 %copy-start.5 = (bf16[128,2560]{1,0:T(8,128)(2,1)S(1)}, bf16[128,2560]{1,0:T(8,128)(2,1)}, u32[]{:S(2)}) copy-start(bf16[128,2560]{1,0:T(8,128)(2,1)} %param.16) | copy-start | bytes 1966084
  65.4 6.7 %copy-start.8 = (f32[2560]{0:T(1024)S(1)}, f32[2560]{0:T(1024)}, u32[]{:S(2)}) copy-start(f32[2560]{0:T(1024)} %param.23) | copy-start | bytes 30724
  71.1 1.1 copy-start.3
  73.2 204.7 %reduce-scatter.2.cloned.1.call-start = ((), (), s32[]{:S(2)}) async-start(), calls=%async_computation.4 | async-start | bytes 11141120 | tf_op jit(solution)/shard_map/reduce_scatter | solution.py:124
  187.8 92.7 %copy-start.1 = (bf16[608,2560]{1,0:T(8,128)(2,1)S(1)}, bf16[608,2560]{1,0:T(8,128)(2,1)}, u32[]{:S(2)}) copy-start(bf16[608,2560]{1,0:T(8,128)(2,1)} %param.26) | copy-start | bytes 9338884
Sparse Core Ops, SparseCore 0:
  73.3 80.9 all-gather.1
  187.9 89.9 reduce-scatter.1
where the time goes:
time: 288 us; the launch traced here: 287 us
  waiting for transfers between devices  187 us (65%)
  matrix products  49.9 us (17%)
  local copies, waits for them, and re-layouts  17.4 us (6%)
  between operations  14.3 us (5%)
  other arithmetic  9.37 us (3%)
  starting transfers between devices  8.92 us (3%)
    reduce_scatter x1, waiting for transfers between devices, shards(): lax.psum_scatter(partial_terms.astype(jnp.bfloat16), 'mlp', scatter_dimen...  89.3 us
    all_gather x1, waiting for transfers between devices, shards(): shard_rows = lax.all_gather(normed, 'mlp', axis=0, tiled=True)  80.9 us
    dot_general x1, matrix products, shards(): jnp.dot(hidden, down_weight, preferred_element_type=jnp.float32)  21.7 us
    dot_general x1, matrix products, shards(): jnp.dot(shard_rows, gate_weight, preferred_element_type=jnp.float32)  11.7 us
    all_to_all x1, waiting for transfers between devices, shards(): lax.all_to_all(send_keys, 'req', split_axis=0, concat_axis=0, tiled=True)  10.7 us
    dot_general x2, matrix products, partial_attention(): jnp.einsum('kgts,skd->tkgd', weights.astype(jnp.bfloat16), value_heads, p...  6.77 us
    all_to_all x1, waiting for transfers between devices, shards(): lax.all_to_all(send_values, 'req', split_axis=0, concat_axis=0, tiled=True)  6.41 us
  transfers between devices with their start and end apart: 4, of which 4 were waited for; matrix products, arithmetic and copies ran while one was open for 4% of the time, Pallas kernels for 0%

commit v1 on v0

--- a/solution.py
+++ b/solution.py
@@ -93,12 +93,11 @@
     positions = jnp.arange(tokens, dtype=jnp.int32)
     causal = positions[:, None] >= positions[None, :]
     local_part = partial_attention(queries, keys_new, values_new, causal)
-    send_keys = jnp.take(slab_keys, sub_block, axis=0)
-    send_values = jnp.take(slab_values, sub_block, axis=0)
-    got_keys, got_values = (
-        lax.all_to_all(send_keys, "req", split_axis=0, concat_axis=0, tiled=True),
-        lax.all_to_all(send_values, "req", split_axis=0, concat_axis=0, tiled=True),
-    )
+    slab_both = jnp.concatenate([slab_keys, slab_values], axis=2)
+    send_both = jnp.take(slab_both, sub_block, axis=0)
+    got_both = lax.all_to_all(send_both, "req", split_axis=0, concat_axis=0, tiled=True)
+    got_keys = got_both[:, :, :width_kv]
+    got_values = got_both[:, :, width_kv:]
     prefix_part = partial_attention(
         queries,
         got_keys.reshape(owners * piece_rows, width_kv),
@@ -116,14 +115,22 @@
         * lax.rsqrt(jnp.mean(widened * widened, axis=1, keepdims=True) + EPSILON)
         * norm_gain[None, :]
     ).astype(jnp.bfloat16)
-    shard_rows = lax.all_gather(normed, "mlp", axis=0, tiled=True)
-    gate_values = jnp.dot(shard_rows, gate_weight, preferred_element_type=jnp.float32)
-    upward = jnp.dot(shard_rows, up_weight, preferred_element_type=jnp.float32)
-    hidden = (jax.nn.silu(gate_values) * upward).astype(jnp.bfloat16)
-    partial_terms = jnp.dot(hidden, down_weight, preferred_element_type=jnp.float32)
-    mixed = lax.psum_scatter(
-        partial_terms.astype(jnp.bfloat16), "mlp", scatter_dimension=0, tiled=True
-    ).astype(jnp.float32)
+    chunks = 2
+    chunk_rows = tokens // chunks
+    mixed_parts = []
+    for part in range(chunks):
+        own_rows = normed[part * chunk_rows:(part + 1) * chunk_rows]
+        shard_rows = lax.all_gather(own_rows, "mlp", axis=0, tiled=True)
+        gate_values = jnp.dot(shard_rows, gate_weight, preferred_element_type=jnp.float32)
+        upward = jnp.dot(shard_rows, up_weight, preferred_element_type=jnp.float32)
+        hidden = (jax.nn.silu(gate_values) * upward).astype(jnp.bfloat16)
+        partial_terms = jnp.dot(hidden, down_weight, preferred_element_type=jnp.float32)
+        mixed_parts.append(
+            lax.psum_scatter(
+                partial_terms.astype(jnp.bfloat16), "mlp", scatter_dimension=0, tiled=True
+            )
+        )
+    mixed = jnp.concatenate(mixed_parts, axis=0).astype(jnp.float32)
     result = residual.astype(jnp.float32) + mixed
     live_slot = positions[:, None] < lengths[0, 0]
     return jnp.where(live_slot, result, 0.0).astype(jnp.bfloat16)

time: 288 us -> 370 us (1.28)
  waiting for transfers between devices: 187 us -> 260 us
  matrix products: 49.9 us -> 58.9 us
  other arithmetic: 9.37 us -> 14.3 us
  starting transfers between devices: 8.92 us -> 4.88 us
    reduce_scatter x1 -> x2, waiting for transfers between devices: 89.3 us -> 144 us  [shards(): lax.psum_scatter(partial_terms.astype(jnp.bfloat16), 'mlp', scatter_dimen...]
    all_gather x1 -> x2, waiting for transfers between devices: 80.9 us -> 93.2 us  [shards(): shard_rows = lax.all_gather(own_rows, 'mlp', axis=0, tiled=True)]
    dot_general x1 -> x2, matrix products: 11.7 us -> 16.6 us  [shards(): jnp.dot(shard_rows, gate_weight, preferred_element_type=jnp.float32)]
    all_to_all x2 -> x1, waiting for transfers between devices: 17.1 us -> 21.9 us  [shards(): lax.all_to_all(send_both, 'req', split_axis=0, concat_axis=0, tiled=True)]
    all_to_all x2 -> x1, starting transfers between devices: 8.65 us -> 4.54 us  [shards(): lax.all_to_all(send_both, 'req', split_axis=0, concat_axis=0, tiled=True)]
    slice x0 -> x2, local copies, waits for them, and re-layouts: none -> 3.97 us  [the longest x1 3.06 us: shards(): got_values = got_both[:, :, width_kv:]]
    dot_general x1 -> x2, matrix products: 21.7 us -> 25.1 us  [shards(): jnp.dot(hidden, down_weight, preferred_element_type=jnp.float32)]
  transfers between devices with their start and end apart: 4 -> 5, of which waited for: 4 -> 5; matrix products, arithmetic and copies ran while one was open for 4% -> 13% of each run, Pallas kernels for 0% -> 0%
where the time goes in v1:
time: 370 us
  waiting for transfers between devices  260 us (70%)
  matrix products  58.9 us (16%)
  local copies, waits for them, and re-layouts  17.7 us (5%)
  other arithmetic  14.3 us (4%)
  between operations  13.9 us (4%)
  starting transfers between devices  4.88 us (1%)
    reduce_scatter x2, waiting for transfers between devices, shards(): lax.psum_scatter(partial_terms.astype(jnp.bfloat16), 'mlp', scatter_dimen...  144 us
    all_gather x2, waiting for transfers between devices, shards(): shard_rows = lax.all_gather(own_rows, 'mlp', axis=0, tiled=True)  93.2 us
    dot_general x2, matrix products, shards(): jnp.dot(hidden, down_weight, preferred_element_type=jnp.float32)  25.1 us
    all_to_all x1, waiting for transfers between devices, shards(): lax.all_to_all(send_both, 'req', split_axis=0, concat_axis=0, tiled=True)  21.9 us
    dot_general x2, matrix products, shards(): jnp.dot(shard_rows, gate_weight, preferred_element_type=jnp.float32)  16.6 us
  transfers between devices with their start and end apart: 5, of which 5 were waited for; matrix products, arithmetic and copies ran while one was open for 13% of the time, Pallas kernels for 0%

profile of v1, /device:TPU:0, one launch (start us, length us, event | category | flops | bytes accessed | tf_op | source)
XLA Modules:
  0.0 369.7 jit_solution(18393647851037582141)
XLA Ops:
  6.5 0.0 copy-start
  6.5 0.8 and_select_fusion
  7.4 0.1 reshape.121
  7.4 0.2 dynamic-slice_reduce_fusion
  7.6 0.9 dynamic-slice_reduce_fusion.1
  8.5 0.1 select_reduce_fusion
  8.6 2.3 pad_maximum_fusion
  10.9 3.2 gather_fusion
  14.1 3.1 broadcast_select_fusion
  17.3 4.5 %all-to-all-start = ((bf16[8,128,1024]{2,1,0:T(8,128)(2,1)}), bf16[8,128,1024]{2,1,0:T(8,128)(2,1)}, u32[]{:S(2)}, u32[]{:S(2)}) async-start(bf16[8,128,1024]{2,1,0:T(8,128)(2,1)} %broadcast_select_fusion), calls=%async_computation | async-start | bytes 4194304 | tf_op jit(solution)/shard_map/all_to_all | solution.py:98
  21.8 0.0 all-gather.3.cloned.1.call-start
  21.8 2.2 reshape.118
  24.1 0.1 copy.47
  24.2 1.4 fusion.35
  25.6 0.2 fusion.17
  25.8 1.4 fusion.19
  27.2 21.9 %all-to-all-done = bf16[8,128,1024]{2,1,0:T(8,128)(2,1)} async-done(((bf16[8,128,1024]{2,1,0:T(8,128)(2,1)}), bf16[8,128,1024]{2,1,0:T(8,128)(2,1)}, u32[]{:S(2)}, u32[]{:S(2)}) %all-to-all-start) | async-done | bytes 2097184 | tf_op jit(solution)/shard_map/all_to_all | solution.py:98
  49.1 3.1 fusion.33
  52.1 2.1 reshape.139
  54.3 5.8 %bitcast_reduce_fusion = (f32[4,4,128]{2,1,0:T(4,128)S(1)}, f32[4,1024,128,4]{2,1,3,0:T(8,128)}) fusion(bf16[128,4,4,128]{3,2,1,0:T(4,128)(2,1)} %reshape.118, bf16[1024,4,128,1]{2,1,0,3:T(4,128)(2,1)} %bitcast.78), kind=kOutput, calls=%fused_computation.2 | convolution fusion | flops 541063168 | bytes 9969664 | tf_op jit(solution)/shard_map/tkgd,skd->kgts/dot_general | solution.py:23
  60.1 2.1 reshape.140
  62.3 4.9 %fusion.1 = f32[4,4,128]{2,1,0:T(4,128)S(1)} fusion(f32[4,1024,128,4]{2,1,3,0:T(8,128)} %get-tuple-element.13, f32[4,4,128]{2,1,0:T(4,128)S(1)} %get-tuple-element.12), kind=kLoop, calls=%fused_computation.4 | loop fusion | flops 6289408 | bytes 8404992 | tf_op jit(solution)/shard_map/reduce_sum | solution.py:30
  67.2 0.9 copy-done.1
  68.0 3.0 fusion.3
  71.0 0.0 copy-start.4
  71.1 0.2 fusion.13
  71.3 0.9 copy-done.4
  72.1 5.6 %multiply_reduce_fusion = (f32[128]{0:T(128)S(1)}, f32[128,2560]{1,0:T(8,128)S(1)}) fusion(bf16[128,2048]{0,1:T(8,128)(2,1)S(1)} %fusion.13, bf16[2048,2560]{1,0:T(8,128)(2,1)} %param.20, bf16[128,2560]{1,0:T(8,128)(2,1)S(1)} %copy-done.4), kind=kOutput, calls=%fused_computation.22 | convolution fusion | flops 1344143232 | bytes 12976640 | tf_op jit(solution)/shard_map/dot_general | solution.py:110
  77.8 1.1 copy-done.2
  78.9 0.0 copy-done.7
  78.9 0.2 multiply_convert_fusion.2
  79.0 0.9 fusion.34
  80.0 0.0 all-gather.3.cloned.1.call-update
  80.0 0.0 all-gather.5.cloned.1.call-start
  80.0 0.7 all-gather.5.cloned.1.call-update
  80.7 0.2 reduce-scatter.3.cloned.1.call-start
  81.0 56.0 %all-gather.3.cloned.1.call-done = bf16[1024,2560]{1,0:T(8,128)(2,1)} async-done(((bf16[64,2560]{1,0:T(8,128)(2,1)}), bf16[1024,2560]{1,0:T(8,128)(2,1)}) %all-gather.3.cloned.1.call-update) | async-done | bytes 5242896 | tf_op jit(solution)/shard_map/all_gather | solution.py:123
  137.0 8.3 %fusion.36 = f32[1024,608]{0,1:T(8,128)} fusion(bf16[1024,2560]{1,0:T(8,128)(2,1)} %all-gather.3.cloned.1.call-done, bf16[2560,608]{0,1:T(8,128)(2,1)} %param.22), kind=kOutput, calls=%fused_computation.66 | convolution fusion | flops 3187671040 | bytes 10846208 | tf_op jit(solution)/shard_map/dot_general | solution.py:124
  145.3 12.6 %convolution_convert_fusion.1 = bf16[1024,2560]{1,0:T(8,128)(2,1)} fusion(bf16[608,2560]{1,0:T(8,128)(2,1)S(1)} %copy-done, f32[1024,608]{0,1:T(8,128)} %fusion.36, bf16[1024,2560]{1,0:T(8,128)(2,1)} %all-gather.3.cloned.1.call-done, bf16[2560,608]{0,1:T(8,128)(2,1)} %param.23), kind=kOutput, calls=%fused_computation.7 | convolution fusion | flops 6381699072 | bytes 19202048 | tf_op jit(solution)/shard_map/dot_general | solution.py:127
  157.9 0.0 reduce-scatter.3.cloned.1.call-update
  157.9 0.0 reduce-scatter.5.cloned.1.call-start
  158.0 37.1 %all-gather.5.cloned.1.call-done = bf16[1024,2560]{1,0:T(8,128)(2,1)} async-done(((bf16[64,2560]{1,0:T(8,128)(2,1)}), bf16[1024,2560]{1,0:T(8,128)(2,1)}) %all-gather.5.cloned.1.call-update) | async-done | bytes 5242896 | tf_op jit(solution)/shard_map/all_gather | solution.py:123
  195.1 8.3 %fusion.37 = f32[1024,608]{0,1:T(8,128)} fusion(bf16[1024,2560]{1,0:T(8,128)(2,1)} %all-gather.5.cloned.1.call-done, bf16[2560,608]{0,1:T(8,128)(2,1)} %param.22), kind=kOutput, calls=%fused_computation.67 | convolution fusion | flops 3187671040 | bytes 10846208 | tf_op jit(solution)/shard_map/dot_general | solution.py:124
  203.4 12.5 %convolution_convert_fusion = bf16[1024,2560]{1,0:T(8,128)(2,1)} fusion(bf16[608,2560]{1,0:T(8,128)(2,1)S(1)} %copy-done, f32[1024,608]{0,1:T(8,128)} %fusion.37, bf16[1024,2560]{1,0:T(8,128)(2,1)} %all-gather.5.cloned.1.call-done, bf16[2560,608]{0,1:T(8,128)(2,1)} %param.23), kind=kOutput, calls=%fused_computation.6 | convolution fusion | flops 6381699072 | bytes 19202048 | tf_op jit(solution)/shard_map/dot_general | solution.py:127
  215.9 0.0 reduce-scatter.5.cloned.1.call-update
  216.6 61.5 %reduce-scatter.3.cloned.1.call-done = bf16[64,2560]{1,0:T(8,128)(2,1)} async-done(((bf16[1024,2560]{1,0:T(8,128)(2,1)}), bf16[64,2560]{1,0:T(8,128)(2,1)}) %reduce-scatter.3.cloned.1.call-update) | async-done | bytes 327696 | tf_op jit(solution)/shard_map/reduce_scatter | solution.py:129
  278.1 82.6 %reduce-scatter.5.cloned.1.call-done = bf16[64,2560]{1,0:T(8,128)(2,1)} async-done(((bf16[1024,2560]{1,0:T(8,128)(2,1)}), bf16[64,2560]{1,0:T(8,128)(2,1)}) %reduce-scatter.5.cloned.1.call-update) | async-done | bytes 327696 | tf_op jit(solution)/shard_map/reduce_scatter | solution.py:129
  360.7 2.5 select_convert_fusion
  (18 shorter events, 0.1 us)
Async XLA Ops:
  6.5 138.8 %copy-start = (bf16[608,2560]{1,0:T(8,128)(2,1)S(1)}, bf16[608,2560]{1,0:T(8,128)(2,1)}, u32[]{:S(2)}) copy-start(bf16[608,2560]{1,0:T(8,128)(2,1)} %param.24) | copy-start | bytes 9338884
  17.2 6.8 %copy-start.5 = (bf16[128,512]{1,0:T(8,128)(2,1)S(1)}, bf16[128,512]{1,0:T(8,128)(2,1)}, u32[]{:S(2)}) copy-start(bf16[128,512]{1,0:T(8,128)(2,1)} %param.16) | copy-start | bytes 393220
  17.3 6.8 %copy-start.6 = (bf16[128,512]{1,0:T(8,128)(2,1)S(1)}, bf16[128,512]{1,0:T(8,128)(2,1)}, u32[]{:S(2)}) copy-start(bf16[128,512]{1,0:T(8,128)(2,1)} %param.17) | copy-start | bytes 393220
  17.3 31.8 %all-to-all-start = ((bf16[8,128,1024]{2,1,0:T(8,128)(2,1)}), bf16[8,128,1024]{2,1,0:T(8,128)(2,1)}, u32[]{:S(2)}, u32[]{:S(2)}) async-start(bf16[8,128,1024]{2,1,0:T(8,128)(2,1)} %broadcast_select_fusion), calls=%async_computation | async-start | bytes 4194304 | tf_op jit(solution)/shard_map/all_to_all | solution.py:98
  21.8 115.2 %all-gather.3.cloned.1.call-start = ((), (), s32[]{:S(2)}) async-start(), calls=%async_computation.3 | async-start | bytes 5570560 | tf_op jit(solution)/shard_map/all_gather | solution.py:123
  62.3 5.8 %copy-start.1 = (f32[4,1024,128,4]{2,1,3,0:T(8,128)S(1)}, f32[4,1024,128,4]{2,1,3,0:T(8,128)}, u32[]{:S(2)}) copy-start(f32[4,1024,128,4]{2,1,3,0:T(8,128)} %get-tuple-element.13) | copy-start | bytes 25165828
  68.0 3.0 copy-start.3
  71.0 1.1 copy-start.4
  72.1 6.7 %copy-start.7 = (f32[2560]{0:T(1024)S(1)}, f32[2560]{0:T(1024)}, u32[]{:S(2)}) copy-start(f32[2560]{0:T(1024)} %param.21) | copy-start | bytes 30724
  77.8 1.1 copy-start.2
  80.0 115.1 %all-gather.5.cloned.1.call-start = ((), (), s32[]{:S(2)}) async-start(), calls=%async_computation.5 | async-start | bytes 5570560 | tf_op jit(solution)/shard_map/all_gather | solution.py:123
  80.7 197.4 %reduce-scatter.3.cloned.1.call-start = ((), (), s32[]{:S(2)}) async-start(), calls=%async_computation.4 | async-start | bytes 5570560 | tf_op jit(solution)/shard_map/reduce_scatter | solution.py:129
  157.9 202.8 %reduce-scatter.5.cloned.1.call-start = ((), (), s32[]{:S(2)}) async-start(), calls=%async_computation.6 | async-start | bytes 5570560 | tf_op jit(solution)/shard_map/reduce_scatter | solution.py:129
Sparse Core Ops, SparseCore 0:
  80.1 56.8 all-gather.2
  139.2 55.8 all-gather.4
  198.5 79.6 reduce-scatter.2
  281.3 79.3 reduce-scatter.4

commit v2 on v0

v2 whole, which is shorter than its diff:
```python
import jax
import jax.numpy as jnp
from jax import lax
from jax.sharding import PartitionSpec as P

HEADS = 16
KVH = 4
HD = 128
GROUPS = 4


NEGATIVE = -1e30
EPSILON = 1e-06


def full_attention(queries, key_rows, value_rows, allowed):
    row_count = queries.shape[0]
    per_group = HEADS // KVH
    outputs = []
    for head in range(KVH):
        query_heads = queries[:, head * per_group * HD:(head + 1) * per_group * HD].reshape(
            row_count, per_group, HD
        )
        key_head = key_rows[:, head * HD:(head + 1) * HD]
        value_head = value_rows[:, head * HD:(head + 1) * HD]
        scores = jnp.einsum(
            "tgd,sd->gts", query_heads, key_head, preferred_element_type=jnp.float32
        ) * HD ** (-0.5)
        scores = jnp.where(allowed[None], scores, NEGATIVE)
        maxima = jnp.max(scores, axis=2, keepdims=True)
        weights = jnp.exp(scores - maxima)
        totals = jnp.sum(weights, axis=2)
        context = jnp.einsum(
            "gts,sd->tgd",
            weights.astype(jnp.bfloat16),
            value_head,
            preferred_element_type=jnp.float32,
        )
        context = context / jnp.transpose(totals)[..., None]
        outputs.append(context.reshape(row_count, per_group * HD))
    return jnp.concatenate(outputs, axis=1).astype(jnp.bfloat16)


def shards(
    hidden_in,
    queries,
    keys_new,
    values_new,
    keys_cache,
    values_cache,
    out_weight,
    norm_gain,
    gate_weight,
    up_weight,
    down_weight,
    lengths,
    slot_request,
    cache_group,
):
    owners = lax.axis_size("req")
    columns = lax.axis_size("mlp")
    owner_index = lax.axis_index("req")
    column_index = lax.axis_index("mlp")
    tokens = queries.shape[0]
    width_kv = keys_cache.shape[1]
    piece_rows = keys_cache.shape[0] // GROUPS
    slot_group = slot_request // (slot_request.shape[0] // GROUPS)
    own_row = cache_group[owner_index]
    wanted = lax.dynamic_slice_in_dim(slot_group.reshape(owners, columns), column_index, 1, 1)[:, 0]
    group_ids = jnp.arange(GROUPS, dtype=jnp.int32)
    sub_block = jnp.sum(
        jnp.where(own_row[None, :] == wanted[:, None], group_ids[None, :], 0), axis=1
    )
    slab_both = jnp.concatenate(
        [keys_cache.reshape(GROUPS, piece_rows, width_kv), values_cache.reshape(GROUPS, piece_rows, width_kv)],
        axis=2,
    )
    pick = (sub_block[:, None] == group_ids[None, :])[:, :, None, None]
    send_both = jnp.sum(jnp.where(pick, slab_both[None], jnp.zeros((), slab_both.dtype)), axis=1)
    got_both = lax.all_to_all(send_both, "req", split_axis=0, concat_axis=0, tiled=True)
    got_both = got_both.reshape(owners * piece_rows, 2 * width_kv)
    key_rows = jnp.concatenate([got_both[:, :width_kv], keys_new], axis=0)
    value_rows = jnp.concatenate([got_both[:, width_kv:], values_new], axis=0)
    positions = jnp.arange(tokens, dtype=jnp.int32)
    causal = positions[:, None] >= positions[None, :]
    allowed = jnp.concatenate(
        [jnp.ones((tokens, owners * piece_rows), jnp.bool_), causal], axis=1
    )
    context = full_attention(queries, key_rows, value_rows, allowed)
    attended = jnp.dot(context, out_weight, preferred_element_type=jnp.float32)
    residual = (hidden_in.astype(jnp.float32) + attended).astype(jnp.bfloat16)
    widened = residual.astype(jnp.float32)
    normed = (
        widened
        * lax.rsqrt(jnp.mean(widened * widened, axis=1, keepdims=True) + EPSILON)
        * norm_gain[None, :]
    ).astype(jnp.bfloat16)
    shard_rows = lax.all_gather(normed, "mlp", axis=0, tiled=True)
    gate_values = jnp.dot(shard_rows, gate_weight, preferred_element_type=jnp.float32)
    upward = jnp.dot(shard_rows, up_weight, preferred_element_type=jnp.float32)
    hidden = (jax.nn.silu(gate_values) * upward).astype(jnp.bfloat16)
    partial_terms = jnp.dot(hidden, down_weight, preferred_element_type=jnp.float32)
    mixed = lax.psum_scatter(
        partial_terms.astype(jnp.bfloat16), "mlp", scatter_dimension=0, tiled=True
    ).astype(jnp.float32)
    result = residual.astype(jnp.float32) + mixed
    live_slot = positions[:, None] < lengths[0, 0]
    return jnp.where(live_slot, result, 0.0).astype(jnp.bfloat16)


def solution(mesh):
    return jax.shard_map(
        shards,
        mesh=mesh,
        in_specs=(
            P(("req", "mlp"), None),
            P(("req", "mlp"), None),
            P(("req", "mlp"), None),
            P(("req", "mlp"), None),
            P("req", None),
            P("req", None),
            P(),
            P(),
            P(None, "mlp"),
            P(None, "mlp"),
            P("mlp", None),
            P("req", "mlp"),
            P(),
            P(),
        ),
        out_specs=P(("req", "mlp"), None),
        check_vma=False,
    )
```

time: 288 us -> 272 us (0.944)
  matrix products: 49.9 us -> 39.2 us
  local copies, waits for them, and re-layouts: 17.4 us -> 10.7 us
  waiting for transfers between devices: 187 us -> 192 us
  starting transfers between devices: 8.92 us -> 4.67 us
    dot_general x4 -> x8, matrix products: 10.8 us -> 4.1 us  [the longest x4 2.24 us: full_attention(): jnp.einsum('gts,sd->tgd', weights.astype(jnp.bfloat16), value_head, prefe...]
    gather x2 -> x0, local copies, waits for them, and re-layouts: 5.3 us -> none  [the longest x1 2.67 us: shards(): send_values = jnp.take(slab_values, sub_block, axis=0)]
    all_to_all x2 -> x1, waiting for transfers between devices: 17.1 us -> 22.1 us  [shards(): lax.all_to_all(send_both, 'req', split_axis=0, concat_axis=0, tiled=True)]
    another operation x2 -> x0, local copies, waits for them, and re-layouts: 4.35 us -> none  [the longest x1 2.21 us: partial_attention(): key_heads = key_rows.reshape(key_count, KVH, HD)]
    all_to_all x2 -> x1, starting transfers between devices: 8.65 us -> 4.41 us  [shards(): lax.all_to_all(send_both, 'req', split_axis=0, concat_axis=0, tiled=True)]
    dot_general x1, matrix products: 5.64 us -> 1.65 us  [shards(): attended = jnp.dot(context, out_weight, preferred_element_type=jnp.float32)]
    slice x0 -> x2, local copies, waits for them, and re-layouts: none -> 3.52 us  [the longest x1 1.81 us: full_attention(): queries[:, head * per_group * HD:(head + 1) * per_group * HD]]
    select_n x2 -> x0, other arithmetic: 3.12 us -> none  [the longest x1 3.12 us: shards(): send_values = jnp.take(slab_values, sub_block, axis=0)]
  transfers between devices with their start and end apart: 4 -> 3, of which waited for: 4 -> 3; matrix products, arithmetic and copies ran while one was open for 4% -> 2% of each run, Pallas kernels for 0% -> 0%
where the time goes in v2:
time: 272 us; the launch traced here: 271 us
  waiting for transfers between devices  192 us (71%)
  matrix products  39.2 us (14%)
  between operations  14.4 us (5%)
  local copies, waits for them, and re-layouts  10.7 us (4%)
  other arithmetic  10 us (4%)
  starting transfers between devices  4.67 us (2%)
    reduce_scatter x1, waiting for transfers between devices, shards(): lax.psum_scatter(partial_terms.astype(jnp.bfloat16), 'mlp', scatter_dimen...  89.4 us
    all_gather x1, waiting for transfers between devices, shards(): shard_rows = lax.all_gather(normed, 'mlp', axis=0, tiled=True)  80.9 us
    all_to_all x1, waiting for transfers between devices, shards(): lax.all_to_all(send_both, 'req', split_axis=0, concat_axis=0, tiled=True)  22.1 us
    dot_general x1, matrix products, shards(): jnp.dot(hidden, down_weight, preferred_element_type=jnp.float32)  21.7 us
    dot_general x1, matrix products, shards(): jnp.dot(shard_rows, gate_weight, preferred_element_type=jnp.float32)  11.7 us
    unnamed x30, local copies, waits for them, and re-layouts  5.97 us
  transfers between devices with their start and end apart: 3, of which 3 were waited for; matrix products, arithmetic and copies ran while one was open for 2% of the time, Pallas kernels for 0%

profile of v2, /device:TPU:0, one launch (start us, length us, event | category | flops | bytes accessed | tf_op | source)
XLA Modules:
  0.0 271.3 jit_solution(10681375120524202327)
XLA Ops:
  6.5 0.8 and_select_fusion
  7.4 0.1 reshape.85
  7.4 0.2 dynamic-slice_reduce_fusion
  7.6 0.9 dynamic-slice_reduce_fusion.1
  8.5 0.1 select_reduce_fusion.1
  8.6 0.1 iota_compare_fusion.1
  8.7 1.3 pad_maximum_fusion
  10.0 2.8 %select_reduce_fusion = bf16[8,128,1024]{2,1,0:T(8,128)(2,1)} fusion(pred[8,4]{1,0:T(8,128)(4,1)S(1)} %iota_compare_fusion.1, bf16[4,128,1024]{2,1,0:T(8,128)(2,1)S(1)} %pad_maximum_fusion), kind=kLoop, calls=%fused_computation.1 | loop fusion | flops 7340032 | bytes 3145760 | tf_op jit(solution)/shard_map/reduce_sum | solution.py:79
  12.8 4.4 %all-to-all-start = ((bf16[8,128,1024]{2,1,0:T(8,128)(2,1)}), bf16[8,128,1024]{2,1,0:T(8,128)(2,1)}, u32[]{:S(2)}, u32[]{:S(2)}) async-start(bf16[8,128,1024]{2,1,0:T(8,128)(2,1)} %select_reduce_fusion), calls=%async_computation | async-start | bytes 4194304 | tf_op jit(solution)/shard_map/all_to_all | solution.py:80
  17.2 0.0 all-gather.2.cloned.1.call-start
  17.3 1.8 fusion.109
  19.1 1.6 copy.71
  20.7 0.7 copy.72
  21.5 0.8 copy.73
  22.2 0.1 copy.74
  22.4 22.1 %all-to-all-done = bf16[8,128,1024]{2,1,0:T(8,128)(2,1)} async-done(((bf16[8,128,1024]{2,1,0:T(8,128)(2,1)}), bf16[8,128,1024]{2,1,0:T(8,128)(2,1)}, u32[]{:S(2)}, u32[]{:S(2)}) %all-to-all-start) | async-done | bytes 2097184 | tf_op jit(solution)/shard_map/all_to_all | solution.py:80
  44.5 1.7 fusion.108
  46.2 0.5 fusion.113
  46.7 0.4 copy-done.7
  47.1 0.5 fusion.112
  47.6 0.3 fusion.11
  47.9 0.3 fusion.13
  48.3 0.2 copy-done.4
  48.5 0.6 fusion.64
  49.1 0.0 slice-start
  49.1 0.6 fusion.61
  49.7 0.3 copy-done.6
  50.0 0.5 fusion.111
  50.4 0.0 slice-start.1
  50.5 0.3 fusion.15
  50.8 0.6 fusion.58
  51.4 0.0 slice-start.2
  51.4 0.5 fusion.110
  51.8 0.3 fusion.17
  52.2 0.6 fusion.55
  52.8 0.1 slice-done.1
  52.9 0.6 slice-done.2
  53.4 1.6 multiply_reduce_fusion
  55.1 1.1 copy-done.2
  56.1 1.0 multiply_convert_fusion.1
  57.1 0.0 all-gather.2.cloned.1.call-update
  57.2 0.2 reduce-scatter.2.cloned.1.call-start
  57.4 80.9 %all-gather.2.cloned.1.call-done = bf16[2048,2560]{1,0:T(8,128)(2,1)} async-done(((bf16[128,2560]{1,0:T(8,128)(2,1)}), bf16[2048,2560]{1,0:T(8,128)(2,1)}) %all-gather.2.cloned.1.call-update) | async-done | bytes 10485776 | tf_op jit(solution)/shard_map/all_gather | solution.py:98
  138.3 11.7 %fusion.114 = f32[2048,608]{0,1:T(8,128)} fusion(bf16[2048,2560]{1,0:T(8,128)(2,1)} %all-gather.2.cloned.1.call-done, bf16[2560,608]{0,1:T(8,128)(2,1)} %param.22), kind=kOutput, calls=%fused_computation.119 | convolution fusion | flops 6375342080 | bytes 18579456 | tf_op jit(solution)/shard_map/dot_general | solution.py:99
  150.0 21.7 %convolution_convert_fusion = bf16[2048,2560]{1,0:T(8,128)(2,1)} fusion(bf16[608,2560]{1,0:T(8,128)(2,1)S(1)} %copy-done, f32[2048,608]{0,1:T(8,128)} %fusion.114, bf16[2048,2560]{1,0:T(8,128)(2,1)} %all-gather.2.cloned.1.call-done, bf16[2560,608]{0,1:T(8,128)(2,1)} %param.23), kind=kOutput, calls=%fused_computation | convolution fusion | flops 12763398144 | bytes 32178176 | tf_op jit(solution)/shard_map/dot_general | solution.py:102
  171.7 0.0 reduce-scatter.2.cloned.1.call-update
  172.6 89.4 %reduce-scatter.2.cloned.1.call-done = bf16[128,2560]{1,0:T(8,128)(2,1)} async-done(((bf16[2048,2560]{1,0:T(8,128)(2,1)}), bf16[128,2560]{1,0:T(8,128)(2,1)}) %reduce-scatter.2.cloned.1.call-update) | async-done | bytes 655376 | tf_op jit(solution)/shard_map/reduce_scatter | solution.py:103
  262.0 2.5 select_convert_fusion
  (22 shorter events, 0.1 us)
Async XLA Ops:
  6.5 143.5 %copy-start = (bf16[608,2560]{1,0:T(8,128)(2,1)S(1)}, bf16[608,2560]{1,0:T(8,128)(2,1)}, u32[]{:S(2)}) copy-start(bf16[608,2560]{1,0:T(8,128)(2,1)} %param.24) | copy-start | bytes 9338884
  12.8 31.7 %all-to-all-start = ((bf16[8,128,1024]{2,1,0:T(8,128)(2,1)}), bf16[8,128,1024]{2,1,0:T(8,128)(2,1)}, u32[]{:S(2)}, u32[]{:S(2)}) async-start(bf16[8,128,1024]{2,1,0:T(8,128)(2,1)} %select_reduce_fusion), calls=%async_computation | async-start | bytes 4194304 | tf_op jit(solution)/shard_map/all_to_all | solution.py:80
  17.2 121.1 %all-gather.2.cloned.1.call-start = ((), (), s32[]{:S(2)}) async-start(), calls=%async_computation.2 | async-start | bytes 11141120 | tf_op jit(solution)/shard_map/all_gather | solution.py:98
  22.2 24.0 %copy-start.3 = (bf16[128,512]{1,0:T(8,128)(2,1)S(1)}, bf16[128,512]{1,0:T(8,128)(2,1)}, u32[]{:S(2)}) copy-start(bf16[128,512]{1,0:T(8,128)(2,1)} %param.16) | copy-start | bytes 393220
  44.5 1.7 copy-start.8
  46.2 0.9 copy-start.7
  47.6 0.9 copy-start.4
  49.1 0.9 copy-start.6
  49.1 3.7 %slice-start = ((s8[10485760]{0:T(1024)(128)(4,1)}), s8[4194304]{0:T(1024)(128)(4,1)S(1)}, s32[]{:S(2)}) async-start(s8[10485760]{0:T(1024)(128)(4,1)} %bitcast.99), calls=%async_computation.4 | async-start | bytes 8388608
  50.4 2.4 slice-start.1
  51.4 2.0 slice-start.2
  52.2 1.2 copy-start.5
  53.4 2.7 %copy-start.9 = (f32[2560]{0:T(1024)S(1)}, f32[2560]{0:T(1024)}, u32[]{:S(2)}) copy-start(f32[2560]{0:T(1024)} %param.21) | copy-start | bytes 30724
  55.1 1.1 copy-start.2
  57.2 204.8 %reduce-scatter.2.cloned.1.call-start = ((), (), s32[]{:S(2)}) async-start(), calls=%async_computation.3 | async-start | bytes 11141120 | tf_op jit(solution)/shard_map/reduce_scatter | solution.py:103
  171.8 92.7 %copy-start.1 = (bf16[608,2560]{1,0:T(8,128)(2,1)S(1)}, bf16[608,2560]{1,0:T(8,128)(2,1)}, u32[]{:S(2)}) copy-start(bf16[608,2560]{1,0:T(8,128)(2,1)} %param.24) | copy-start | bytes 9338884
Sparse Core Ops, SparseCore 0:
  57.3 80.9 all-gather.1
  171.9 90.0 reduce-scatter.1

commit v3 on v2

--- a/solution.py
+++ b/solution.py
@@ -96,8 +96,11 @@
         * norm_gain[None, :]
     ).astype(jnp.bfloat16)
     shard_rows = lax.all_gather(normed, "mlp", axis=0, tiled=True)
-    gate_values = jnp.dot(shard_rows, gate_weight, preferred_element_type=jnp.float32)
-    upward = jnp.dot(shard_rows, up_weight, preferred_element_type=jnp.float32)
+    block_width = gate_weight.shape[1]
+    both_weights = jnp.concatenate([gate_weight, up_weight], axis=1)
+    both_values = jnp.dot(shard_rows, both_weights, preferred_element_type=jnp.float32)
+    gate_values = both_values[:, :block_width]
+    upward = both_values[:, block_width:]
     hidden = (jax.nn.silu(gate_values) * upward).astype(jnp.bfloat16)
     partial_terms = jnp.dot(hidden, down_weight, preferred_element_type=jnp.float32)
     mixed = lax.psum_scatter(

time: 272 us -> 267 us (0.982)
  matrix products: 39.2 us -> 34.1 us
    dot_general x1, matrix products: 21.7 us -> 11.1 us  [shards(): jnp.dot(hidden, down_weight, preferred_element_type=jnp.float32)]
    dot_general x1, matrix products: 11.7 us -> 17.2 us  [shards(): jnp.dot(shard_rows, both_weights, preferred_element_type=jnp.float32)]
    unnamed x30 -> x28, local copies, waits for them, and re-layouts: 5.97 us -> 5.97 us
where the time goes in v3:
time: 267 us; the launch traced here: 266 us
  waiting for transfers between devices  193 us (72%)
  matrix products  34.1 us (13%)
  between operations  14.3 us (5%)
  local copies, waits for them, and re-layouts  10.7 us (4%)
  other arithmetic  10 us (4%)
  starting transfers between devices  4.67 us (2%)
    reduce_scatter x1, waiting for transfers between devices, shards(): lax.psum_scatter(partial_terms.astype(jnp.bfloat16), 'mlp', scatter_dimen...  89.7 us
    all_gather x1, waiting for transfers between devices, shards(): shard_rows = lax.all_gather(normed, 'mlp', axis=0, tiled=True)  80.9 us
    all_to_all x1, waiting for transfers between devices, shards(): lax.all_to_all(send_both, 'req', split_axis=0, concat_axis=0, tiled=True)  22.1 us
    dot_general x1, matrix products, shards(): jnp.dot(shard_rows, both_weights, preferred_element_type=jnp.float32)  17.2 us
    dot_general x1, matrix products, shards(): jnp.dot(hidden, down_weight, preferred_element_type=jnp.float32)  11.1 us
    unnamed x28, local copies, waits for them, and re-layouts  5.97 us
  transfers between devices with their start and end apart: 3, of which 3 were waited for; matrix products, arithmetic and copies ran while one was open for 2% of the time, Pallas kernels for 0%

profile of v3, /device:TPU:0, one launch (start us, length us, event | category | flops | bytes accessed | tf_op | source)
XLA Modules:
  0.0 266.4 jit_solution(3412705867624227788)
XLA Ops:
  6.5 0.8 and_select_fusion
  7.4 0.1 reshape.85
  7.4 0.2 dynamic-slice_reduce_fusion
  7.6 0.9 dynamic-slice_reduce_fusion.1
  8.5 0.1 select_reduce_fusion.1
  8.6 0.1 iota_compare_fusion.1
  8.7 1.3 pad_maximum_fusion
  10.0 2.8 %select_reduce_fusion = bf16[8,128,1024]{2,1,0:T(8,128)(2,1)} fusion(pred[8,4]{1,0:T(8,128)(4,1)S(1)} %iota_compare_fusion.1, bf16[4,128,1024]{2,1,0:T(8,128)(2,1)S(1)} %pad_maximum_fusion), kind=kLoop, calls=%fused_computation.1 | loop fusion | flops 7340032 | bytes 3145760 | tf_op jit(solution)/shard_map/reduce_sum | solution.py:79
  12.8 4.4 %all-to-all-start = ((bf16[8,128,1024]{2,1,0:T(8,128)(2,1)}), bf16[8,128,1024]{2,1,0:T(8,128)(2,1)}, u32[]{:S(2)}, u32[]{:S(2)}) async-start(bf16[8,128,1024]{2,1,0:T(8,128)(2,1)} %select_reduce_fusion), calls=%async_computation | async-start | bytes 4194304 | tf_op jit(solution)/shard_map/all_to_all | solution.py:80
  17.2 0.0 all-gather.2.cloned.1.call-start
  17.3 1.8 fusion.116
  19.1 1.6 copy.71
  20.7 0.7 copy.72
  21.5 0.8 copy.73
  22.2 0.1 copy.74
  22.4 22.1 %all-to-all-done = bf16[8,128,1024]{2,1,0:T(8,128)(2,1)} async-done(((bf16[8,128,1024]{2,1,0:T(8,128)(2,1)}), bf16[8,128,1024]{2,1,0:T(8,128)(2,1)}, u32[]{:S(2)}, u32[]{:S(2)}) %all-to-all-start) | async-done | bytes 2097184 | tf_op jit(solution)/shard_map/all_to_all | solution.py:80
  44.5 1.7 fusion.115
  46.2 0.5 fusion.120
  46.7 0.4 copy-done.6
  47.1 0.5 fusion.119
  47.6 0.3 fusion.17
  47.9 0.3 fusion.19
  48.3 0.2 copy-done.3
  48.5 0.6 fusion.70
  49.1 0.0 slice-start
  49.1 0.6 fusion.67
  49.7 0.3 copy-done.5
  50.0 0.5 fusion.118
  50.4 0.0 slice-start.1
  50.5 0.3 fusion.21
  50.8 0.6 fusion.64
  51.4 0.0 slice-start.2
  51.4 0.5 fusion.117
  51.8 0.3 fusion.23
  52.2 0.6 fusion.61
  52.8 0.1 slice-done.1
  52.9 0.6 slice-done.2
  53.4 1.6 multiply_reduce_fusion
  55.1 1.1 copy-done.1
  56.1 1.0 multiply_convert_fusion
  57.2 0.0 all-gather.2.cloned.1.call-update
  57.2 0.2 reduce-scatter.2.cloned.1.call-start
  57.4 80.9 %all-gather.2.cloned.1.call-done = bf16[2048,2560]{1,0:T(8,128)(2,1)} async-done(((bf16[128,2560]{1,0:T(8,128)(2,1)}), bf16[2048,2560]{1,0:T(8,128)(2,1)}) %all-gather.2.cloned.1.call-update) | async-done | bytes 10485776 | tf_op jit(solution)/shard_map/all_gather | solution.py:98
  138.3 17.2 %fusion = f32[2048,1216]{0,1:T(8,128)S(1)} fusion(bf16[2048,2560]{1,0:T(8,128)(2,1)} %all-gather.2.cloned.1.call-done, bf16[2560,608]{0,1:T(8,128)(2,1)} %param.23, bf16[2560,608]{0,1:T(8,128)(2,1)} %param.22), kind=kOutput, calls=%fused_computation.2 | convolution fusion | flops 12763136000 | bytes 26673152 | tf_op jit(solution)/shard_map/dot_general | solution.py:101
  155.5 11.1 %convolution_convert_fusion = bf16[2048,2560]{1,0:T(8,128)(2,1)} fusion(bf16[608,2560]{1,0:T(8,128)(2,1)S(1)} %copy-done, f32[2048,1216]{0,1:T(8,128)S(1)} %fusion), kind=kOutput, calls=%fused_computation | convolution fusion | flops 6388056064 | bytes 23560192 | tf_op jit(solution)/shard_map/dot_general | solution.py:105
  166.6 0.0 reduce-scatter.2.cloned.1.call-update
  167.3 89.7 %reduce-scatter.2.cloned.1.call-done = bf16[128,2560]{1,0:T(8,128)(2,1)} async-done(((bf16[2048,2560]{1,0:T(8,128)(2,1)}), bf16[128,2560]{1,0:T(8,128)(2,1)}) %reduce-scatter.2.cloned.1.call-update) | async-done | bytes 655376 | tf_op jit(solution)/shard_map/reduce_scatter | solution.py:106
  257.1 2.5 select_convert_fusion
  (20 shorter events, 0.1 us)
Async XLA Ops:
  6.5 149.0 %copy-start = (bf16[608,2560]{1,0:T(8,128)(2,1)S(1)}, bf16[608,2560]{1,0:T(8,128)(2,1)}, u32[]{:S(2)}) copy-start(bf16[608,2560]{1,0:T(8,128)(2,1)} %param.24) | copy-start | bytes 9338884
  12.8 31.7 %all-to-all-start = ((bf16[8,128,1024]{2,1,0:T(8,128)(2,1)}), bf16[8,128,1024]{2,1,0:T(8,128)(2,1)}, u32[]{:S(2)}, u32[]{:S(2)}) async-start(bf16[8,128,1024]{2,1,0:T(8,128)(2,1)} %select_reduce_fusion), calls=%async_computation | async-start | bytes 4194304 | tf_op jit(solution)/shard_map/all_to_all | solution.py:80
  17.2 121.1 %all-gather.2.cloned.1.call-start = ((), (), s32[]{:S(2)}) async-start(), calls=%async_computation.2 | async-start | bytes 11141120 | tf_op jit(solution)/shard_map/all_gather | solution.py:98
  22.2 24.0 %copy-start.2 = (bf16[128,512]{1,0:T(8,128)(2,1)S(1)}, bf16[128,512]{1,0:T(8,128)(2,1)}, u32[]{:S(2)}) copy-start(bf16[128,512]{1,0:T(8,128)(2,1)} %param.16) | copy-start | bytes 393220
  44.5 1.7 copy-start.7
  46.2 0.9 copy-start.6
  47.6 0.9 copy-start.3
  49.1 0.9 copy-start.5
  49.1 3.7 %slice-start = ((s8[10485760]{0:T(1024)(128)(4,1)}), s8[4194304]{0:T(1024)(128)(4,1)S(1)}, s32[]{:S(2)}) async-start(s8[10485760]{0:T(1024)(128)(4,1)} %bitcast.96), calls=%async_computation.4 | async-start | bytes 8388608
  50.4 2.4 slice-start.1
  51.4 2.0 slice-start.2
  52.2 1.2 copy-start.4
  53.4 2.7 %copy-start.8 = (f32[2560]{0:T(1024)S(1)}, f32[2560]{0:T(1024)}, u32[]{:S(2)}) copy-start(f32[2560]{0:T(1024)} %param.21) | copy-start | bytes 30724
  55.1 1.1 copy-start.1
  57.2 199.9 %reduce-scatter.2.cloned.1.call-start = ((), (), s32[]{:S(2)}) async-start(), calls=%async_computation.3 | async-start | bytes 11141120 | tf_op jit(solution)/shard_map/reduce_scatter | solution.py:106
Sparse Core Ops, SparseCore 0:
  57.3 80.9 all-gather.1
  166.8 90.2 reduce-scatter.1

commit v4 on v3

--- a/solution.py
+++ b/solution.py
@@ -64,19 +64,20 @@
     tokens = queries.shape[0]
     width_kv = keys_cache.shape[1]
     piece_rows = keys_cache.shape[0] // GROUPS
-    slot_group = slot_request // (slot_request.shape[0] // GROUPS)
+    slot_group = lax.div(slot_request, slot_request.shape[0] // GROUPS)
     own_row = cache_group[owner_index]
     wanted = lax.dynamic_slice_in_dim(slot_group.reshape(owners, columns), column_index, 1, 1)[:, 0]
     group_ids = jnp.arange(GROUPS, dtype=jnp.int32)
     sub_block = jnp.sum(
         jnp.where(own_row[None, :] == wanted[:, None], group_ids[None, :], 0), axis=1
     )
-    slab_both = jnp.concatenate(
-        [keys_cache.reshape(GROUPS, piece_rows, width_kv), values_cache.reshape(GROUPS, piece_rows, width_kv)],
-        axis=2,
-    )
+    slab_keys = keys_cache.reshape(GROUPS, piece_rows, width_kv)
+    slab_values = values_cache.reshape(GROUPS, piece_rows, width_kv)
     pick = (sub_block[:, None] == group_ids[None, :])[:, :, None, None]
-    send_both = jnp.sum(jnp.where(pick, slab_both[None], jnp.zeros((), slab_both.dtype)), axis=1)
+    zero = jnp.zeros((), keys_cache.dtype)
+    send_keys = sum(jnp.where(pick[:, j], slab_keys[j][None], zero) for j in range(GROUPS))
+    send_values = sum(jnp.where(pick[:, j], slab_values[j][None], zero) for j in range(GROUPS))
+    send_both = jnp.concatenate([send_keys, send_values], axis=2)
     got_both = lax.all_to_all(send_both, "req", split_axis=0, concat_axis=0, tiled=True)
     got_both = got_both.reshape(owners * piece_rows, 2 * width_kv)
     key_rows = jnp.concatenate([got_both[:, :width_kv], keys_new], axis=0)

time: 267 us -> 266 us (level)
    reduce_sum x1 -> x0, other arithmetic: 2.85 us -> none  [shards(): jnp.sum(jnp.where(pick, slab_both[None], jnp.zeros((), slab_both.dtype)),...]
where the time goes in v4:
time: 266 us
  waiting for transfers between devices  192 us (72%)
  matrix products  34.1 us (13%)
  between operations  14.3 us (5%)
  local copies, waits for them, and re-layouts  12.1 us (5%)
  other arithmetic  7.91 us (3%)
  starting transfers between devices  4.67 us (2%)
    reduce_scatter x1, waiting for transfers between devices, shards(): lax.psum_scatter(partial_terms.astype(jnp.bfloat16), 'mlp', scatter_dimen...  89.5 us
    all_gather x1, waiting for transfers between devices, shards(): shard_rows = lax.all_gather(normed, 'mlp', axis=0, tiled=True)  80.9 us
    all_to_all x1, waiting for transfers between devices, shards(): lax.all_to_all(send_both, 'req', split_axis=0, concat_axis=0, tiled=True)  22.1 us
    dot_general x1, matrix products, shards(): jnp.dot(shard_rows, both_weights, preferred_element_type=jnp.float32)  17.2 us
    dot_general x1, matrix products, shards(): jnp.dot(hidden, down_weight, preferred_element_type=jnp.float32)  11.1 us
    unnamed x28, local copies, waits for them, and re-layouts  5.97 us
  transfers between devices with their start and end apart: 3, of which 3 were waited for; matrix products, arithmetic and copies ran while one was open for 2% of the time, Pallas kernels for 0%

profile of v4, /device:TPU:0, one launch (start us, length us, event | category | flops | bytes accessed | tf_op | source)
XLA Modules:
  0.0 265.5 jit_solution(2752284598802310465)
XLA Ops:
  6.5 0.8 compare_select_fusion
  7.3 0.1 reshape.110
  7.4 0.2 dynamic-slice_reduce_fusion
  7.6 0.9 dynamic-slice_reduce_fusion.1
  8.5 0.1 select_reduce_fusion
  8.6 1.4 fusion.118
  10.0 0.6 select_add_fusion.1
  10.6 1.6 pad_maximum_fusion
  12.1 4.4 %all-to-all-start = ((bf16[8,128,1024]{2,1,0:T(8,128)(2,1)}), bf16[8,128,1024]{2,1,0:T(8,128)(2,1)}, u32[]{:S(2)}, u32[]{:S(2)}) async-start(bf16[8,128,1024]{2,1,0:T(8,128)(2,1)} %pad_maximum_fusion), calls=%async_computation | async-start | bytes 4194304 | tf_op jit(solution)/shard_map/all_to_all | solution.py:81
  16.5 0.0 all-gather.2.cloned.1.call-start
  16.6 1.8 fusion.117
  18.4 1.6 copy.71
  20.0 0.7 copy.72
  20.8 0.8 copy.73
  21.5 0.1 copy.74
  21.7 22.1 %all-to-all-done = bf16[8,128,1024]{2,1,0:T(8,128)(2,1)} async-done(((bf16[8,128,1024]{2,1,0:T(8,128)(2,1)}), bf16[8,128,1024]{2,1,0:T(8,128)(2,1)}, u32[]{:S(2)}, u32[]{:S(2)}) %all-to-all-start) | async-done | bytes 2097184 | tf_op jit(solution)/shard_map/all_to_all | solution.py:81
  43.8 1.7 fusion.116
  45.6 0.5 fusion.123
  46.0 0.4 copy-done.6
  46.4 0.5 fusion.122
  46.9 0.3 fusion.17
  47.2 0.3 fusion.19
  47.6 0.2 copy-done.3
  47.8 0.6 fusion.70
  48.4 0.0 slice-start
  48.4 0.6 fusion.67
  49.0 0.3 copy-done.5
  49.3 0.5 fusion.121
  49.8 0.0 slice-start.1
  49.8 0.3 fusion.21
  50.1 0.6 fusion.64
  50.7 0.0 slice-start.2
  50.7 0.5 fusion.120
  51.2 0.3 fusion.23
  51.5 0.6 fusion.61
  52.1 0.1 slice-done.1
  52.2 0.6 slice-done.2
  52.7 1.6 multiply_reduce_fusion
  54.4 1.1 copy-done.1
  55.5 1.0 multiply_convert_fusion
  56.5 0.0 all-gather.2.cloned.1.call-update
  56.5 0.2 reduce-scatter.2.cloned.1.call-start
  56.7 80.9 %all-gather.2.cloned.1.call-done = bf16[2048,2560]{1,0:T(8,128)(2,1)} async-done(((bf16[128,2560]{1,0:T(8,128)(2,1)}), bf16[2048,2560]{1,0:T(8,128)(2,1)}) %all-gather.2.cloned.1.call-update) | async-done | bytes 10485776 | tf_op jit(solution)/shard_map/all_gather | solution.py:99
  137.6 17.2 %fusion = f32[2048,1216]{0,1:T(8,128)S(1)} fusion(bf16[2048,2560]{1,0:T(8,128)(2,1)} %all-gather.2.cloned.1.call-done, bf16[2560,608]{0,1:T(8,128)(2,1)} %param.23, bf16[2560,608]{0,1:T(8,128)(2,1)} %param.22), kind=kOutput, calls=%fused_computation.1 | convolution fusion | flops 12763136000 | bytes 26673152 | tf_op jit(solution)/shard_map/dot_general | solution.py:102
  154.8 11.1 %convolution_convert_fusion = bf16[2048,2560]{1,0:T(8,128)(2,1)} fusion(bf16[608,2560]{1,0:T(8,128)(2,1)S(1)} %copy-done, f32[2048,1216]{0,1:T(8,128)S(1)} %fusion), kind=kOutput, calls=%fused_computation | convolution fusion | flops 6388056064 | bytes 23560192 | tf_op jit(solution)/shard_map/dot_general | solution.py:106
  166.0 0.0 reduce-scatter.2.cloned.1.call-update
  166.7 89.5 %reduce-scatter.2.cloned.1.call-done = bf16[128,2560]{1,0:T(8,128)(2,1)} async-done(((bf16[2048,2560]{1,0:T(8,128)(2,1)}), bf16[128,2560]{1,0:T(8,128)(2,1)}) %reduce-scatter.2.cloned.1.call-update) | async-done | bytes 655376 | tf_op jit(solution)/shard_map/reduce_scatter | solution.py:107
  256.1 2.5 select_convert_fusion
  (22 shorter events, 0.1 us)
Async XLA Ops:
  6.5 148.3 %copy-start = (bf16[608,2560]{1,0:T(8,128)(2,1)S(1)}, bf16[608,2560]{1,0:T(8,128)(2,1)}, u32[]{:S(2)}) copy-start(bf16[608,2560]{1,0:T(8,128)(2,1)} %param.24) | copy-start | bytes 9338884
  12.1 31.7 %all-to-all-start = ((bf16[8,128,1024]{2,1,0:T(8,128)(2,1)}), bf16[8,128,1024]{2,1,0:T(8,128)(2,1)}, u32[]{:S(2)}, u32[]{:S(2)}) async-start(bf16[8,128,1024]{2,1,0:T(8,128)(2,1)} %pad_maximum_fusion), calls=%async_computation | async-start | bytes 4194304 | tf_op jit(solution)/shard_map/all_to_all | solution.py:81
  16.5 121.1 %all-gather.2.cloned.1.call-start = ((), (), s32[]{:S(2)}) async-start(), calls=%async_computation.2 | async-start | bytes 11141120 | tf_op jit(solution)/shard_map/all_gather | solution.py:99
  21.5 24.0 %copy-start.2 = (bf16[128,512]{1,0:T(8,128)(2,1)S(1)}, bf16[128,512]{1,0:T(8,128)(2,1)}, u32[]{:S(2)}) copy-start(bf16[128,512]{1,0:T(8,128)(2,1)} %param.16) | copy-start | bytes 393220
  43.8 1.7 copy-start.7
  45.5 0.9 copy-start.6
  46.9 0.9 copy-start.3
  48.4 0.9 copy-start.5
  48.4 3.7 %slice-start = ((s8[10485760]{0:T(1024)(128)(4,1)}), s8[4194304]{0:T(1024)(128)(4,1)S(1)}, s32[]{:S(2)}) async-start(s8[10485760]{0:T(1024)(128)(4,1)} %bitcast.102), calls=%async_computation.4 | async-start | bytes 8388608
  49.8 2.4 slice-start.1
  50.7 2.0 slice-start.2
  51.5 1.2 copy-start.4
  52.7 2.7 %copy-start.8 = (f32[2560]{0:T(1024)S(1)}, f32[2560]{0:T(1024)}, u32[]{:S(2)}) copy-start(f32[2560]{0:T(1024)} %param.21) | copy-start | bytes 30724
  54.4 1.1 copy-start.1
  56.5 199.7 %reduce-scatter.2.cloned.1.call-start = ((), (), s32[]{:S(2)}) async-start(), calls=%async_computation.3 | async-start | bytes 11141120 | tf_op jit(solution)/shard_map/reduce_scatter | solution.py:107
Sparse Core Ops, SparseCore 0:
  56.6 80.9 all-gather.1
  166.1 89.9 reduce-scatter.1

commit v5 on v4

--- a/solution.py
+++ b/solution.py
@@ -77,11 +77,14 @@
     zero = jnp.zeros((), keys_cache.dtype)
     send_keys = sum(jnp.where(pick[:, j], slab_keys[j][None], zero) for j in range(GROUPS))
     send_values = sum(jnp.where(pick[:, j], slab_values[j][None], zero) for j in range(GROUPS))
-    send_both = jnp.concatenate([send_keys, send_values], axis=2)
+    send_both = jnp.concatenate([send_keys, send_values], axis=1)
     got_both = lax.all_to_all(send_both, "req", split_axis=0, concat_axis=0, tiled=True)
-    got_both = got_both.reshape(owners * piece_rows, 2 * width_kv)
-    key_rows = jnp.concatenate([got_both[:, :width_kv], keys_new], axis=0)
-    value_rows = jnp.concatenate([got_both[:, width_kv:], values_new], axis=0)
+    key_rows = jnp.concatenate(
+        [got_both[:, :piece_rows].reshape(owners * piece_rows, width_kv), keys_new], axis=0
+    )
+    value_rows = jnp.concatenate(
+        [got_both[:, piece_rows:].reshape(owners * piece_rows, width_kv), values_new], axis=0
+    )
     positions = jnp.arange(tokens, dtype=jnp.int32)
     causal = positions[:, None] >= positions[None, :]
     allowed = jnp.concatenate(
@@ -107,9 +110,10 @@
     mixed = lax.psum_scatter(
         partial_terms.astype(jnp.bfloat16), "mlp", scatter_dimension=0, tiled=True
     ).astype(jnp.float32)
-    result = residual.astype(jnp.float32) + mixed
     live_slot = positions[:, None] < lengths[0, 0]
-    return jnp.where(live_slot, result, 0.0).astype(jnp.bfloat16)
+    kept = jnp.where(live_slot, residual.astype(jnp.float32), 0.0)
+    live_scale = live_slot.astype(jnp.float32)
+    return (kept + live_scale * mixed).astype(jnp.bfloat16)
 
 
 def solution(mesh):

time: 266 us -> 270 us (1.015)
  local copies, waits for them, and re-layouts: 12.1 us -> 17.6 us
    unnamed x28 -> x31, local copies, waits for them, and re-layouts: 5.97 us -> 7.92 us
  transfers between devices with their start and end apart: 3 -> 3, of which waited for: 3 -> 3; matrix products, arithmetic and copies ran while one was open for 2% -> 3% of each run, Pallas kernels for 0% -> 0%
where the time goes in v5:
time: 270 us
  waiting for transfers between devices  190 us (70%)
  matrix products  35.1 us (13%)
  local copies, waits for them, and re-layouts  17.6 us (7%)
  between operations  14.3 us (5%)
  other arithmetic  7.89 us (3%)
  starting transfers between devices  4.67 us (2%)
    reduce_scatter x1, waiting for transfers between devices, shards(): lax.psum_scatter(partial_terms.astype(jnp.bfloat16), 'mlp', scatter_dimen...  89 us
    all_gather x1, waiting for transfers between devices, shards(): shard_rows = lax.all_gather(normed, 'mlp', axis=0, tiled=True)  80.9 us
    all_to_all x1, waiting for transfers between devices, shards(): lax.all_to_all(send_both, 'req', split_axis=0, concat_axis=0, tiled=True)  20.4 us
    dot_general x1, matrix products, shards(): jnp.dot(shard_rows, both_weights, preferred_element_type=jnp.float32)  17.2 us
    dot_general x1, matrix products, shards(): jnp.dot(hidden, down_weight, preferred_element_type=jnp.float32)  11.1 us
    unnamed x31, local copies, waits for them, and re-layouts  7.92 us
  transfers between devices with their start and end apart: 3, of which 3 were waited for; matrix products, arithmetic and copies ran while one was open for 3% of the time, Pallas kernels for 0%

profile of v5, /device:TPU:0, one launch (start us, length us, event | category | flops | bytes accessed | tf_op | source)
XLA Modules:
  0.0 269.9 jit_solution(10644022984411775870)
XLA Ops:
  6.5 0.8 compare_select_fusion
  7.3 0.1 reshape.116
  7.4 0.2 dynamic-slice_reduce_fusion
  7.6 0.9 dynamic-slice_reduce_fusion.1
  8.5 0.1 select_reduce_fusion
  8.6 1.4 fusion.119
  10.0 0.6 select_add_fusion.1
  10.6 1.4 pad_maximum_fusion
  12.0 4.4 %all-to-all-start = ((bf16[8,256,512]{2,1,0:T(8,128)(2,1)}), bf16[8,256,512]{2,1,0:T(8,128)(2,1)}, u32[]{:S(2)}, u32[]{:S(2)}) async-start(bf16[8,256,512]{2,1,0:T(8,128)(2,1)} %pad_maximum_fusion), calls=%async_computation | async-start | bytes 4194304 | tf_op jit(solution)/shard_map/all_to_all | solution.py:81
  16.4 0.0 all-gather.2.cloned.1.call-start
  16.5 1.8 fusion.118
  18.3 0.8 copy.58
  19.0 1.0 copy.36
  20.0 1.6 copy.59
  21.7 0.7 copy.60
  22.4 0.8 copy.61
  23.3 20.4 %all-to-all-done = bf16[8,256,512]{2,1,0:T(8,128)(2,1)} async-done(((bf16[8,256,512]{2,1,0:T(8,128)(2,1)}), bf16[8,256,512]{2,1,0:T(8,128)(2,1)}, u32[]{:S(2)}, u32[]{:S(2)}) %all-to-all-start) | async-done | bytes 2097184 | tf_op jit(solution)/shard_map/all_to_all | solution.py:81
  43.7 3.0 %fusion.117 = (bf16[8,128,512]{2,1,0:T(8,128)(2,1)}, bf16[8,128,512]{2,1,0:T(8,128)(2,1)}) fusion(bf16[8,256,512]{2,1,0:T(8,128)(2,1)} %all-to-all-done), kind=kLoop, calls=%fused_computation.124 | loop fusion | bytes 4194304 | tf_op jit(solution)/shard_map/slice | solution.py:86
  46.7 2.3 copy.57
  49.0 1.6 fusion.124
  50.6 0.5 fusion.123
  51.1 0.3 fusion.17
  51.4 0.3 fusion.19
  51.7 0.6 copy-done.2
  52.3 0.5 fusion.70
  52.8 0.5 fusion.67
  53.4 0.3 copy-done.7
  53.7 0.5 fusion.122
  54.2 0.0 slice-start.1
  54.2 0.3 fusion.21
  54.5 0.5 fusion.64
  55.1 0.5 copy-done.6
  55.6 0.5 fusion.121
  56.1 0.3 fusion.23
  56.4 0.5 fusion.61
  57.0 0.5 slice-done.2
  57.4 0.1 copy-done.5
  57.5 1.6 multiply_reduce_fusion
  59.2 1.1 copy-done.3
  60.2 1.0 multiply_convert_fusion
  61.2 0.0 all-gather.2.cloned.1.call-update
  61.3 0.2 reduce-scatter.2.cloned.1.call-start
  61.5 80.9 %all-gather.2.cloned.1.call-done = bf16[2048,2560]{1,0:T(8,128)(2,1)} async-done(((bf16[128,2560]{1,0:T(8,128)(2,1)}), bf16[2048,2560]{1,0:T(8,128)(2,1)}) %all-gather.2.cloned.1.call-update) | async-done | bytes 10485776 | tf_op jit(solution)/shard_map/all_gather | solution.py:102
  142.4 17.2 %fusion = f32[2048,1216]{0,1:T(8,128)S(1)} fusion(bf16[2048,2560]{1,0:T(8,128)(2,1)} %all-gather.2.cloned.1.call-done, bf16[2560,608]{0,1:T(8,128)(2,1)} %param.23, bf16[2560,608]{0,1:T(8,128)(2,1)} %param.22), kind=kOutput, calls=%fused_computation.1 | convolution fusion | flops 12763136000 | bytes 26673152 | tf_op jit(solution)/shard_map/dot_general | solution.py:105
  159.6 11.1 %convolution_convert_fusion = bf16[2048,2560]{1,0:T(8,128)(2,1)} fusion(bf16[608,2560]{1,0:T(8,128)(2,1)S(1)} %copy-done, f32[2048,1216]{0,1:T(8,128)S(1)} %fusion), kind=kOutput, calls=%fused_computation | convolution fusion | flops 6388056064 | bytes 23560192 | tf_op jit(solution)/shard_map/dot_general | solution.py:109
  170.7 0.0 reduce-scatter.2.cloned.1.call-update
  171.4 89.0 %reduce-scatter.2.cloned.1.call-done = bf16[128,2560]{1,0:T(8,128)(2,1)} async-done(((bf16[2048,2560]{1,0:T(8,128)(2,1)}), bf16[128,2560]{1,0:T(8,128)(2,1)}) %reduce-scatter.2.cloned.1.call-update) | async-done | bytes 655376 | tf_op jit(solution)/shard_map/reduce_scatter | solution.py:110
  260.4 2.6 add_convert_fusion
  (26 shorter events, 0.1 us)
Async XLA Ops:
  6.5 153.1 %copy-start = (bf16[608,2560]{1,0:T(8,128)(2,1)S(1)}, bf16[608,2560]{1,0:T(8,128)(2,1)}, u32[]{:S(2)}) copy-start(bf16[608,2560]{1,0:T(8,128)(2,1)} %param.24) | copy-start | bytes 9338884
  12.0 31.7 %all-to-all-start = ((bf16[8,256,512]{2,1,0:T(8,128)(2,1)}), bf16[8,256,512]{2,1,0:T(8,128)(2,1)}, u32[]{:S(2)}, u32[]{:S(2)}) async-start(bf16[8,256,512]{2,1,0:T(8,128)(2,1)} %pad_maximum_fusion), calls=%async_computation | async-start | bytes 4194304 | tf_op jit(solution)/shard_map/all_to_all | solution.py:81
  16.4 126.0 %all-gather.2.cloned.1.call-start = ((), (), s32[]{:S(2)}) async-start(), calls=%async_computation.2 | async-start | bytes 11141120 | tf_op jit(solution)/shard_map/all_gather | solution.py:102
  23.3 25.7 %copy-start.4 = (bf16[128,512]{1,0:T(8,128)(2,1)S(1)}, bf16[128,512]{1,0:T(8,128)(2,1)}, u32[]{:S(2)}) copy-start(bf16[128,512]{1,0:T(8,128)(2,1)} %param.16) | copy-start | bytes 393220
  49.0 1.6 copy-start.1
  49.0 1.6 copy-start.8
  51.0 1.2 copy-start.2
  52.8 0.9 copy-start.7
  52.8 4.1 %slice-start = ((s8[10485760]{0:T(1024)(128)(4,1)}), s8[4194304]{0:T(1024)(128)(4,1)S(1)}, s32[]{:S(2)}) async-start(s8[10485760]{0:T(1024)(128)(4,1)} %bitcast.107), calls=%async_computation.4 | async-start | bytes 8388608
  54.2 2.8 %slice-start.1 = ((s8[10485760]{0:T(1024)(128)(4,1)}), s8[4194304]{0:T(1024)(128)(4,1)S(1)}, s32[]{:S(2)}) async-start(s8[10485760]{0:T(1024)(128)(4,1)} %bitcast.107), calls=%async_computation.5 | async-start | bytes 8388608
  54.5 1.1 copy-start.6
  55.6 1.8 slice-start.2
  56.4 1.1 copy-start.5
  57.5 2.7 %copy-start.9 = (f32[2560]{0:T(1024)S(1)}, f32[2560]{0:T(1024)}, u32[]{:S(2)}) copy-start(f32[2560]{0:T(1024)} %param.21) | copy-start | bytes 30724
  59.1 1.1 copy-start.3
  61.3 199.2 %reduce-scatter.2.cloned.1.call-start = ((), (), s32[]{:S(2)}) async-start(), calls=%async_computation.3 | async-start | bytes 11141120 | tf_op jit(solution)/shard_map/reduce_scatter | solution.py:110
Sparse Core Ops, SparseCore 0:
  61.4 80.9 all-gather.1
  170.9 89.5 reduce-scatter.1

commit v6 on v4

--- a/solution.py
+++ b/solution.py
@@ -13,27 +13,33 @@
 EPSILON = 1e-06
 
 
-def full_attention(queries, key_rows, value_rows, allowed):
+def full_attention(queries, prefix_keys, prefix_values, keys_new, values_new, causal):
     row_count = queries.shape[0]
     per_group = HEADS // KVH
     outputs = []
     for head in range(KVH):
+        columns = slice(head * HD, (head + 1) * HD)
         query_heads = queries[:, head * per_group * HD:(head + 1) * per_group * HD].reshape(
             row_count, per_group, HD
         )
-        key_head = key_rows[:, head * HD:(head + 1) * HD]
-        value_head = value_rows[:, head * HD:(head + 1) * HD]
-        scores = jnp.einsum(
-            "tgd,sd->gts", query_heads, key_head, preferred_element_type=jnp.float32
+        scores_new = jnp.einsum(
+            "tgd,sd->gts", query_heads, keys_new[:, columns], preferred_element_type=jnp.float32
         ) * HD ** (-0.5)
-        scores = jnp.where(allowed[None], scores, NEGATIVE)
-        maxima = jnp.max(scores, axis=2, keepdims=True)
-        weights = jnp.exp(scores - maxima)
-        totals = jnp.sum(weights, axis=2)
+        scores_new = jnp.where(causal[None], scores_new, NEGATIVE)
+        scores_old = jnp.einsum(
+            "tgd,sd->gts", query_heads, prefix_keys[:, columns], preferred_element_type=jnp.float32
+        ) * HD ** (-0.5)
+        maxima = jnp.maximum(
+            jnp.max(scores_new, axis=2, keepdims=True), jnp.max(scores_old, axis=2, keepdims=True)
+        )
+        weights_new = jnp.exp(scores_new - maxima)
+        weights_old = jnp.exp(scores_old - maxima)
+        totals = jnp.sum(weights_new, axis=2) + jnp.sum(weights_old, axis=2)
         context = jnp.einsum(
-            "gts,sd->tgd",
-            weights.astype(jnp.bfloat16),
-            value_head,
+            "gts,sd->tgd", weights_old.astype(jnp.bfloat16), prefix_values[:, columns],
+            preferred_element_type=jnp.float32,
+        ) + jnp.einsum(
+            "gts,sd->tgd", weights_new.astype(jnp.bfloat16), values_new[:, columns],
             preferred_element_type=jnp.float32,
         )
         context = context / jnp.transpose(totals)[..., None]
@@ -80,14 +86,11 @@
     send_both = jnp.concatenate([send_keys, send_values], axis=2)
     got_both = lax.all_to_all(send_both, "req", split_axis=0, concat_axis=0, tiled=True)
     got_both = got_both.reshape(owners * piece_rows, 2 * width_kv)
-    key_rows = jnp.concatenate([got_both[:, :width_kv], keys_new], axis=0)
-    value_rows = jnp.concatenate([got_both[:, width_kv:], values_new], axis=0)
     positions = jnp.arange(tokens, dtype=jnp.int32)
     causal = positions[:, None] >= positions[None, :]
-    allowed = jnp.concatenate(
-        [jnp.ones((tokens, owners * piece_rows), jnp.bool_), causal], axis=1
+    context = full_attention(
+        queries, got_both[:, :width_kv], got_both[:, width_kv:], keys_new, values_new, causal
     )
-    context = full_attention(queries, key_rows, value_rows, allowed)
     attended = jnp.dot(context, out_weight, preferred_element_type=jnp.float32)
     residual = (hidden_in.astype(jnp.float32) + attended).astype(jnp.bfloat16)
     widened = residual.astype(jnp.float32)

time: 266 us -> 272 us (1.023)
  matrix products: 34.1 us -> 49.5 us
  waiting for transfers between devices: 192 us -> 187 us
  local copies, waits for them, and re-layouts: 12.1 us -> 7.61 us
    dot_general x8 -> x16, matrix products: 4.1 us -> 19.5 us  [the longest x4 6.7 us: full_attention(): jnp.einsum('tgd,sd->gts', query_heads, keys_new[:, columns], preferred_el...]
    all_to_all x1, waiting for transfers between devices: 22.1 us -> 16.7 us  [shards(): lax.all_to_all(send_both, 'req', split_axis=0, concat_axis=0, tiled=True)]
  transfers between devices with their start and end apart: 3 -> 3, of which waited for: 3 -> 3; matrix products, arithmetic and copies ran while one was open for 2% -> 4% of each run, Pallas kernels for 0% -> 0%
where the time goes in v6:
time: 272 us; the launch traced here: 271 us
  waiting for transfers between devices  187 us (69%)
  matrix products  49.5 us (18%)
  between operations  14.4 us (5%)
  other arithmetic  8.32 us (3%)
  local copies, waits for them, and re-layouts  7.61 us (3%)
  starting transfers between devices  4.67 us (2%)
    reduce_scatter x1, waiting for transfers between devices, shards(): lax.psum_scatter(partial_terms.astype(jnp.bfloat16), 'mlp', scatter_dimen...  89.4 us
    all_gather x1, waiting for transfers between devices, shards(): shard_rows = lax.all_gather(normed, 'mlp', axis=0, tiled=True)  80.9 us
    dot_general x1, matrix products, shards(): jnp.dot(shard_rows, both_weights, preferred_element_type=jnp.float32)  17.2 us
    all_to_all x1, waiting for transfers between devices, shards(): lax.all_to_all(send_both, 'req', split_axis=0, concat_axis=0, tiled=True)  16.7 us
    dot_general x1, matrix products, shards(): jnp.dot(hidden, down_weight, preferred_element_type=jnp.float32)  11.1 us
    dot_general x4, matrix products, full_attention(): jnp.einsum('tgd,sd->gts', query_heads, keys_new[:, columns], preferred_el...  6.7 us
    dot_general x4, matrix products, full_attention(): jnp.einsum('gts,sd->tgd', weights_old.astype(jnp.bfloat16), prefix_values...  6.22 us
    dot_general x4, matrix products, full_attention(): jnp.einsum('tgd,sd->gts', query_heads, prefix_keys[:, columns], preferred...  5.71 us
  transfers between devices with their start and end apart: 3, of which 3 were waited for; matrix products, arithmetic and copies ran while one was open for 4% of the time, Pallas kernels for 0%

profile of v6, /device:TPU:0, one launch (start us, length us, event | category | flops | bytes accessed | tf_op | source)
XLA Modules:
  0.0 271.5 jit_solution(8414097394037358727)
XLA Ops:
  6.5 0.8 compare_select_fusion
  7.3 0.1 reshape.141
  7.4 0.2 dynamic-slice_reduce_fusion
  7.6 0.9 dynamic-slice_reduce_fusion.1
  8.5 0.1 select_reduce_fusion
  8.6 1.4 fusion.105
  10.0 0.6 select_add_fusion.1
  10.6 1.6 pad_maximum_fusion
  12.1 4.4 %all-to-all-start = ((bf16[8,128,1024]{2,1,0:T(8,128)(2,1)}), bf16[8,128,1024]{2,1,0:T(8,128)(2,1)}, u32[]{:S(2)}, u32[]{:S(2)}) async-start(bf16[8,128,1024]{2,1,0:T(8,128)(2,1)} %pad_maximum_fusion), calls=%async_computation | async-start | bytes 4194304 | tf_op jit(solution)/shard_map/all_to_all | solution.py:87
  16.6 1.8 fusion.104
  18.4 0.8 copy.111
  19.1 0.1 copy.113
  19.3 0.1 copy.115
  19.4 1.0 copy.117
  20.4 1.8 fusion.110
  22.2 1.6 fusion.109
  23.9 1.6 fusion.108
  25.5 1.6 fusion.107
  27.1 16.7 %all-to-all-done = bf16[8,128,1024]{2,1,0:T(8,128)(2,1)} async-done(((bf16[8,128,1024]{2,1,0:T(8,128)(2,1)}), bf16[8,128,1024]{2,1,0:T(8,128)(2,1)}, u32[]{:S(2)}, u32[]{:S(2)}) %all-to-all-start) | async-done | bytes 2097184 | tf_op jit(solution)/shard_map/all_to_all | solution.py:87
  43.8 1.4 bitcast_reduce_fusion.3
  45.2 0.4 fusion.13
  45.6 1.5 convolution_bitcast_fusion.7
  47.1 1.4 bitcast_reduce_fusion.2
  48.5 0.4 fusion.15
  48.8 1.5 convolution_bitcast_fusion.6
  50.3 1.5 bitcast_reduce_fusion.1
  51.9 0.4 fusion.17
  52.3 1.6 convolution_bitcast_fusion.5
  53.9 1.4 bitcast_reduce_fusion
  55.3 0.4 fusion.19
  55.7 1.6 convolution_bitcast_fusion.4
  57.4 0.1 fusion.64
  57.4 0.1 fusion.66
  57.6 0.1 fusion.70
  57.7 0.2 fusion.37
  57.9 0.2 fusion.38
  58.1 0.2 fusion.39
  58.4 0.2 fusion.40
  58.6 0.1 copy-done.6
  58.8 1.6 multiply_reduce_fusion
  60.4 1.1 copy-done.1
  61.5 1.0 multiply_convert_fusion
  62.5 0.2 reduce-scatter.2.cloned.1.call-start
  62.8 80.9 %all-gather.2.cloned.1.call-done = bf16[2048,2560]{1,0:T(8,128)(2,1)} async-done(((bf16[128,2560]{1,0:T(8,128)(2,1)}), bf16[2048,2560]{1,0:T(8,128)(2,1)}) %all-gather.2.cloned.1.call-update) | async-done | bytes 10485776 | tf_op jit(solution)/shard_map/all_gather | solution.py:102
  143.7 17.2 %fusion = f32[2048,1216]{0,1:T(8,128)S(1)} fusion(bf16[2048,2560]{1,0:T(8,128)(2,1)} %all-gather.2.cloned.1.call-done, bf16[2560,608]{0,1:T(8,128)(2,1)} %param.23, bf16[2560,608]{0,1:T(8,128)(2,1)} %param.22), kind=kOutput, calls=%fused_computation.1 | convolution fusion | flops 12763136000 | bytes 26673152 | tf_op jit(solution)/shard_map/dot_general | solution.py:105
  160.9 11.1 %convolution_convert_fusion = bf16[2048,2560]{1,0:T(8,128)(2,1)} fusion(bf16[608,2560]{1,0:T(8,128)(2,1)S(1)} %copy-done, f32[2048,1216]{0,1:T(8,128)S(1)} %fusion), kind=kOutput, calls=%fused_computation | convolution fusion | flops 6388056064 | bytes 23560192 | tf_op jit(solution)/shard_map/dot_general | solution.py:109
  172.7 89.4 %reduce-scatter.2.cloned.1.call-done = bf16[128,2560]{1,0:T(8,128)(2,1)} async-done(((bf16[2048,2560]{1,0:T(8,128)(2,1)}), bf16[128,2560]{1,0:T(8,128)(2,1)}) %reduce-scatter.2.cloned.1.call-update) | async-done | bytes 655376 | tf_op jit(solution)/shard_map/reduce_scatter | solution.py:110
  262.1 2.5 select_convert_fusion
  (40 shorter events, 0.3 us)
Async XLA Ops:
  6.5 154.3 %copy-start = (bf16[608,2560]{1,0:T(8,128)(2,1)S(1)}, bf16[608,2560]{1,0:T(8,128)(2,1)}, u32[]{:S(2)}) copy-start(bf16[608,2560]{1,0:T(8,128)(2,1)} %param.24) | copy-start | bytes 9338884
  12.1 31.7 %all-to-all-start = ((bf16[8,128,1024]{2,1,0:T(8,128)(2,1)}), bf16[8,128,1024]{2,1,0:T(8,128)(2,1)}, u32[]{:S(2)}, u32[]{:S(2)}) async-start(bf16[8,128,1024]{2,1,0:T(8,128)(2,1)} %pad_maximum_fusion), calls=%async_computation | async-start | bytes 4194304 | tf_op jit(solution)/shard_map/all_to_all | solution.py:87
  16.5 127.1 %all-gather.2.cloned.1.call-start = ((), (), s32[]{:S(2)}) async-start(), calls=%async_computation.2 | async-start | bytes 11141120 | tf_op jit(solution)/shard_map/all_gather | solution.py:102
  50.3 8.3 %slice-start = ((s8[10485760]{0:T(1024)(128)(4,1)}), s8[4194304]{0:T(1024)(128)(4,1)S(1)}, s32[]{:S(2)}) async-start(s8[10485760]{0:T(1024)(128)(4,1)} %bitcast.202), calls=%async_computation.4 | async-start | bytes 8388608
  52.2 6.4 %slice-start.1 = ((s8[10485760]{0:T(1024)(128)(4,1)}), s8[4194304]{0:T(1024)(128)(4,1)S(1)}, s32[]{:S(2)}) async-start(s8[10485760]{0:T(1024)(128)(4,1)} %bitcast.202), calls=%async_computation.5 | async-start | bytes 8388608
  55.3 2.1 copy-start.5
  55.3 2.1 copy-start.4
  55.7 1.8 copy-start.3
  55.7 1.9 copy-start.2
  55.7 2.0 copy-start.8
  55.7 2.9 %slice-start.2 = ((s8[10485760]{0:T(1024)(128)(4,1)}), s8[2097152]{0:T(1024)(128)(4,1)S(1)}, s32[]{:S(2)}) async-start(s8[10485760]{0:T(1024)(128)(4,1)} %bitcast.202), calls=%async_computation.6 | async-start | bytes 4194304
  57.7 1.1 copy-start.6
  58.8 2.7 %copy-start.7 = (f32[2560]{0:T(1024)S(1)}, f32[2560]{0:T(1024)}, u32[]{:S(2)}) copy-start(f32[2560]{0:T(1024)} %param.21) | copy-start | bytes 30724
  60.4 1.1 copy-start.1
  62.5 199.6 %reduce-scatter.2.cloned.1.call-start = ((), (), s32[]{:S(2)}) async-start(), calls=%async_computation.3 | async-start | bytes 11141120 | tf_op jit(solution)/shard_map/reduce_scatter | solution.py:110
Sparse Core Ops, SparseCore 0:
  62.7 80.9 all-gather.1
  172.2 89.9 reduce-scatter.1

commit v7 on v5

--- a/solution.py
+++ b/solution.py
@@ -77,13 +77,13 @@
     zero = jnp.zeros((), keys_cache.dtype)
     send_keys = sum(jnp.where(pick[:, j], slab_keys[j][None], zero) for j in range(GROUPS))
     send_values = sum(jnp.where(pick[:, j], slab_values[j][None], zero) for j in range(GROUPS))
-    send_both = jnp.concatenate([send_keys, send_values], axis=1)
-    got_both = lax.all_to_all(send_both, "req", split_axis=0, concat_axis=0, tiled=True)
+    got_keys = lax.all_to_all(send_keys, "req", split_axis=0, concat_axis=0, tiled=True)
+    got_values = lax.all_to_all(send_values, "req", split_axis=0, concat_axis=0, tiled=True)
     key_rows = jnp.concatenate(
-        [got_both[:, :piece_rows].reshape(owners * piece_rows, width_kv), keys_new], axis=0
+        [got_keys.reshape(owners * piece_rows, width_kv), keys_new], axis=0
     )
     value_rows = jnp.concatenate(
-        [got_both[:, piece_rows:].reshape(owners * piece_rows, width_kv), values_new], axis=0
+        [got_values.reshape(owners * piece_rows, width_kv), values_new], axis=0
     )
     positions = jnp.arange(tokens, dtype=jnp.int32)
     causal = positions[:, None] >= positions[None, :]
@@ -110,10 +110,9 @@
     mixed = lax.psum_scatter(
         partial_terms.astype(jnp.bfloat16), "mlp", scatter_dimension=0, tiled=True
     ).astype(jnp.float32)
+    result = residual.astype(jnp.float32) + mixed
     live_slot = positions[:, None] < lengths[0, 0]
-    kept = jnp.where(live_slot, residual.astype(jnp.float32), 0.0)
-    live_scale = live_slot.astype(jnp.float32)
-    return (kept + live_scale * mixed).astype(jnp.bfloat16)
+    return jnp.where(live_slot, result, 0.0).astype(jnp.bfloat16)
 
 
 def solution(mesh):

time: 270 us -> 277 us (1.026)
  blocking collectives: 0 us -> 20.3 us
  waiting for transfers between devices: 190 us -> 176 us
  matrix products: 35.1 us -> 38.4 us
    all_to_all x0 -> x1, blocking collectives: none -> 20.3 us  [shards(): lax.all_to_all(send_values, 'req', split_axis=0, concat_axis=0, tiled=True)]
    all_to_all x1, waiting for transfers between devices: 20.4 us -> 5.85 us  [shards(): lax.all_to_all(send_keys, 'req', split_axis=0, concat_axis=0, tiled=True)]
    dot_general x4, matrix products: 2.94 us -> 6.29 us  [full_attention(): jnp.einsum('tgd,sd->gts', query_heads, key_head, preferred_element_type=j...]
    slice x2 -> x1, local copies, waits for them, and re-layouts: 4.41 us -> 1.39 us  [shards(): slab_values[j][None]]
    unnamed x31 -> x29, local copies, waits for them, and re-layouts: 7.92 us -> 8.82 us
  transfers between devices with their start and end apart: 3 -> 3, of which waited for: 3 -> 3; matrix products, arithmetic and copies ran while one was open for 3% -> 4% of each run, Pallas kernels for 0% -> 0%
where the time goes in v7:
time: 277 us; the launch traced here: 276 us
  waiting for transfers between devices  176 us (64%)
  matrix products  38.4 us (14%)
  blocking collectives  20.3 us (7%)
  local copies, waits for them, and re-layouts  15.5 us (6%)
  between operations  14.3 us (5%)
  other arithmetic  7.4 us (3%)
  starting transfers between devices  4.49 us (2%)
    reduce_scatter x1, waiting for transfers between devices, shards(): lax.psum_scatter(partial_terms.astype(jnp.bfloat16), 'mlp', scatter_dimen...  89.2 us
    all_gather x1, waiting for transfers between devices, shards(): shard_rows = lax.all_gather(normed, 'mlp', axis=0, tiled=True)  80.9 us
    all_to_all x1, blocking collectives, shards(): lax.all_to_all(send_values, 'req', split_axis=0, concat_axis=0, tiled=True)  20.3 us
    dot_general x1, matrix products, shards(): jnp.dot(shard_rows, both_weights, preferred_element_type=jnp.float32)  17.2 us
    dot_general x1, matrix products, shards(): jnp.dot(hidden, down_weight, preferred_element_type=jnp.float32)  11.1 us
    unnamed x29, local copies, waits for them, and re-layouts  8.82 us
    dot_general x4, matrix products, full_attention(): jnp.einsum('tgd,sd->gts', query_heads, key_head, preferred_element_type=j...  6.29 us
    all_to_all x1, waiting for transfers between devices, shards(): lax.all_to_all(send_keys, 'req', split_axis=0, concat_axis=0, tiled=True)  5.85 us
  transfers between devices with their start and end apart: 3, of which 3 were waited for; matrix products, arithmetic and copies ran while one was open for 4% of the time, Pallas kernels for 0%

profile of v7, /device:TPU:0, one launch (start us, length us, event | category | flops | bytes accessed | tf_op | source)
XLA Modules:
  0.0 276.3 jit_solution(2070619221559886263)
XLA Ops:
  6.5 0.8 compare_select_fusion
  7.3 0.1 reshape.113
  7.4 0.2 dynamic-slice_reduce_fusion
  7.6 0.9 dynamic-slice_reduce_fusion.1
  8.5 0.1 select_reduce_fusion
  8.6 1.4 fusion.117
  10.0 1.6 select_add_fusion.1
  11.6 20.3 %all_to_all.10 = bf16[8,128,512]{2,1,0:T(8,128)(2,1)} all-to-all(bf16[8,128,512]{2,1,0:T(8,128)(2,1)S(1)} %get-tuple-element.17), channel_id=1, replica_groups=mesh['req'=8,'mlp'=16] {'req'}, dimensions={0} | all-to-all | bytes 2097152 | tf_op jit(solution)/shard_map/all_to_all | solution.py:81
  31.9 4.2 %all-to-all-start.1 = ((bf16[8,128,512]{2,1,0:T(8,128)(2,1)}), bf16[8,128,512]{2,1,0:T(8,128)(2,1)}, u32[]{:S(2)}, u32[]{:S(2)}) async-start(bf16[8,128,512]{2,1,0:T(8,128)(2,1)} %get-tuple-element.18), calls=%async_computation.1 | async-start | bytes 2097152 | tf_op jit(solution)/shard_map/all_to_all | solution.py:80
  36.1 0.0 copy-start.3
  36.1 0.0 all-gather.2.cloned.1.call-start
  36.2 1.8 fusion.116
  38.0 0.8 copy.58
  38.8 1.0 copy.36
  39.8 1.6 copy.59
  41.4 1.7 copy.60
  43.1 0.8 copy.61
  43.9 2.3 copy.57
  46.2 5.9 %all-to-all-done.1 = bf16[8,128,512]{2,1,0:T(8,128)(2,1)} async-done(((bf16[8,128,512]{2,1,0:T(8,128)(2,1)}), bf16[8,128,512]{2,1,0:T(8,128)(2,1)}, u32[]{:S(2)}, u32[]{:S(2)}) %all-to-all-start.1) | async-done | bytes 1048608 | tf_op jit(solution)/shard_map/all_to_all | solution.py:80
  52.1 1.5 fusion.122
  53.6 1.4 fusion.121
  55.0 0.3 fusion.17
  55.3 0.3 fusion.19
  55.6 0.6 copy-done.1
  56.2 0.5 fusion.70
  56.7 0.0 slice-start
  56.8 0.5 fusion.67
  57.3 0.3 copy-done.6
  57.6 1.8 fusion.120
  59.5 0.0 slice-start.1
  59.5 0.3 fusion.21
  59.8 0.5 fusion.64
  60.4 0.5 copy-done.5
  60.9 1.6 fusion.119
  62.5 0.3 fusion.23
  62.8 0.5 fusion.61
  63.4 0.5 copy-done.4
  63.9 1.6 multiply_reduce_fusion
  65.6 1.1 copy-done.2
  66.6 1.0 multiply_convert_fusion
  67.6 0.0 all-gather.2.cloned.1.call-update
  67.7 0.2 reduce-scatter.2.cloned.1.call-start
  67.9 80.9 %all-gather.2.cloned.1.call-done = bf16[2048,2560]{1,0:T(8,128)(2,1)} async-done(((bf16[128,2560]{1,0:T(8,128)(2,1)}), bf16[2048,2560]{1,0:T(8,128)(2,1)}) %all-gather.2.cloned.1.call-update) | async-done | bytes 10485776 | tf_op jit(solution)/shard_map/all_gather | solution.py:102
  148.8 17.2 %fusion = f32[2048,1216]{0,1:T(8,128)S(1)} fusion(bf16[2048,2560]{1,0:T(8,128)(2,1)} %all-gather.2.cloned.1.call-done, bf16[2560,608]{0,1:T(8,128)(2,1)} %param.23, bf16[2560,608]{0,1:T(8,128)(2,1)} %param.22), kind=kOutput, calls=%fused_computation.1 | convolution fusion | flops 12763136000 | bytes 26673152 | tf_op jit(solution)/shard_map/dot_general | solution.py:105
  166.0 11.1 %convolution_convert_fusion = bf16[2048,2560]{1,0:T(8,128)(2,1)} fusion(bf16[608,2560]{1,0:T(8,128)(2,1)S(1)} %copy-done, f32[2048,1216]{0,1:T(8,128)S(1)} %fusion), kind=kOutput, calls=%fused_computation | convolution fusion | flops 6388056064 | bytes 23560192 | tf_op jit(solution)/shard_map/dot_general | solution.py:109
  177.1 0.0 reduce-scatter.2.cloned.1.call-update
  177.8 89.2 %reduce-scatter.2.cloned.1.call-done = bf16[128,2560]{1,0:T(8,128)(2,1)} async-done(((bf16[2048,2560]{1,0:T(8,128)(2,1)}), bf16[128,2560]{1,0:T(8,128)(2,1)}) %reduce-scatter.2.cloned.1.call-update) | async-done | bytes 655376 | tf_op jit(solution)/shard_map/reduce_scatter | solution.py:110
  267.0 2.5 select_convert_fusion
  (23 shorter events, 0.1 us)
Async XLA Ops:
  6.5 159.5 %copy-start = (bf16[608,2560]{1,0:T(8,128)(2,1)S(1)}, bf16[608,2560]{1,0:T(8,128)(2,1)}, u32[]{:S(2)}) copy-start(bf16[608,2560]{1,0:T(8,128)(2,1)} %param.24) | copy-start | bytes 9338884
  31.9 20.2 %all-to-all-start.1 = ((bf16[8,128,512]{2,1,0:T(8,128)(2,1)}), bf16[8,128,512]{2,1,0:T(8,128)(2,1)}, u32[]{:S(2)}, u32[]{:S(2)}) async-start(bf16[8,128,512]{2,1,0:T(8,128)(2,1)} %get-tuple-element.18), calls=%async_computation.1 | async-start | bytes 2097152 | tf_op jit(solution)/shard_map/all_to_all | solution.py:80
  36.1 15.9 %copy-start.3 = (bf16[128,512]{1,0:T(8,128)(2,1)S(1)}, bf16[128,512]{1,0:T(8,128)(2,1)}, u32[]{:S(2)}) copy-start(bf16[128,512]{1,0:T(8,128)(2,1)} %param.16) | copy-start | bytes 393220
  36.1 112.6 %all-gather.2.cloned.1.call-start = ((), (), s32[]{:S(2)}) async-start(), calls=%async_computation.3 | async-start | bytes 11141120 | tf_op jit(solution)/shard_map/all_gather | solution.py:102
  52.0 1.5 copy-start.7
  55.0 1.2 copy-start.1
  56.7 0.9 copy-start.6
  56.7 6.6 %slice-start = ((s8[10485760]{0:T(1024)(128)(4,1)}), s8[4194304]{0:T(1024)(128)(4,1)S(1)}, s32[]{:S(2)}) async-start(s8[10485760]{0:T(1024)(128)(4,1)} %bitcast.103), calls=%async_computation.5 | async-start | bytes 8388608
  59.5 3.9 %slice-start.1 = ((s8[10485760]{0:T(1024)(128)(4,1)}), s8[4194304]{0:T(1024)(128)(4,1)S(1)}, s32[]{:S(2)}) async-start(s8[10485760]{0:T(1024)(128)(4,1)} %bitcast.103), calls=%async_computation.6 | async-start | bytes 8388608
  59.8 1.1 copy-start.5
  60.9 2.5 slice-start.2
  62.8 1.1 copy-start.4
  63.9 2.7 copy-start.8
  65.5 1.1 copy-start.2
  67.7 199.3 %reduce-scatter.2.cloned.1.call-start = ((), (), s32[]{:S(2)}) async-start(), calls=%async_computation.4 | async-start | bytes 11141120 | tf_op jit(solution)/shard_map/reduce_scatter | solution.py:110
Sparse Core Ops, SparseCore 0:
  67.8 80.9 all-gather.1
  177.3 89.6 reduce-scatter.1

commit v8 on v3

--- a/solution.py
+++ b/solution.py
@@ -64,7 +64,7 @@
     tokens = queries.shape[0]
     width_kv = keys_cache.shape[1]
     piece_rows = keys_cache.shape[0] // GROUPS
-    slot_group = slot_request // (slot_request.shape[0] // GROUPS)
+    slot_group = lax.div(slot_request, slot_request.shape[0] // GROUPS)
     own_row = cache_group[owner_index]
     wanted = lax.dynamic_slice_in_dim(slot_group.reshape(owners, columns), column_index, 1, 1)[:, 0]
     group_ids = jnp.arange(GROUPS, dtype=jnp.int32)
@@ -75,8 +75,9 @@
         [keys_cache.reshape(GROUPS, piece_rows, width_kv), values_cache.reshape(GROUPS, piece_rows, width_kv)],
         axis=2,
     )
-    pick = (sub_block[:, None] == group_ids[None, :])[:, :, None, None]
-    send_both = jnp.sum(jnp.where(pick, slab_both[None], jnp.zeros((), slab_both.dtype)), axis=1)
+    send_both = jnp.stack(
+        [lax.dynamic_index_in_dim(slab_both, sub_block[r], 0, keepdims=False) for r in range(owners)]
+    )
     got_both = lax.all_to_all(send_both, "req", split_axis=0, concat_axis=0, tiled=True)
     got_both = got_both.reshape(owners * piece_rows, 2 * width_kv)
     key_rows = jnp.concatenate([got_both[:, :width_kv], keys_new], axis=0)

time: 267 us -> 292 us (1.094)
  between operations: 14.3 us -> 29.1 us
  other arithmetic: 10 us -> 19.4 us
    unnamed x1 -> x8, other arithmetic: 0.01 us -> 11.9 us
where the time goes in v8:
time: 292 us; the launch traced here: 291 us
  waiting for transfers between devices  192 us (66%)
  matrix products  34.1 us (12%)
  between operations  29.1 us (10%)
  other arithmetic  19.4 us (7%)
  local copies, waits for them, and re-layouts  11.3 us (4%)
  starting transfers between devices  4.67 us (2%)
    reduce_scatter x1, waiting for transfers between devices, shards(): lax.psum_scatter(partial_terms.astype(jnp.bfloat16), 'mlp', scatter_dimen...  89.5 us
    all_gather x1, waiting for transfers between devices, shards(): shard_rows = lax.all_gather(normed, 'mlp', axis=0, tiled=True)  80.9 us
    all_to_all x1, waiting for transfers between devices, shards(): lax.all_to_all(send_both, 'req', split_axis=0, concat_axis=0, tiled=True)  22.1 us
    dot_general x1, matrix products, shards(): jnp.dot(shard_rows, both_weights, preferred_element_type=jnp.float32)  17.2 us
    unnamed x8, other arithmetic  11.9 us
    dot_general x1, matrix products, shards(): jnp.dot(hidden, down_weight, preferred_element_type=jnp.float32)  11.1 us
    unnamed x28, local copies, waits for them, and re-layouts  5.97 us
  transfers between devices with their start and end apart: 3, of which 3 were waited for; matrix products, arithmetic and copies ran while one was open for 2% of the time, Pallas kernels for 0%

profile of v8, /device:TPU:0, one launch (start us, length us, event | category | flops | bytes accessed | tf_op | source)
XLA Modules:
  0.0 291.1 jit_solution(15349829835590367867)
XLA Ops:
  6.5 0.8 compare_select_fusion
  7.3 0.1 reshape.65
  7.4 0.2 fusion.120
  7.6 0.9 fusion.121
  8.5 0.1 select_reduce_fusion
  8.6 0.7 fusion.136
  20.3 1.7 fusion.107
  22.0 1.7 fusion.109
  24.4 1.7 fusion.111
  26.7 1.7 fusion.113
  29.0 1.7 fusion.115
  31.3 1.7 fusion.117
  33.7 1.7 fusion.119
  36.1 1.7 fusion.105
  37.8 4.4 %all-to-all-start = ((bf16[8,128,1024]{2,1,0:T(8,128)(2,1)}), bf16[8,128,1024]{2,1,0:T(8,128)(2,1)}, u32[]{:S(2)}, u32[]{:S(2)}) async-start(bf16[8,128,1024]{2,1,0:T(8,128)(2,1)} %fusion.105), calls=%async_computation | async-start | bytes 4194304 | tf_op jit(solution)/shard_map/all_to_all | solution.py:81
  42.2 1.8 fusion.135
  44.0 1.6 copy.71
  45.7 0.7 copy.72
  46.4 0.8 copy.73
  47.2 0.1 copy.74
  47.4 22.1 %all-to-all-done = bf16[8,128,1024]{2,1,0:T(8,128)(2,1)} async-done(((bf16[8,128,1024]{2,1,0:T(8,128)(2,1)}), bf16[8,128,1024]{2,1,0:T(8,128)(2,1)}, u32[]{:S(2)}, u32[]{:S(2)}) %all-to-all-start) | async-done | bytes 2097184 | tf_op jit(solution)/shard_map/all_to_all | solution.py:81
  69.5 1.7 fusion.134
  71.2 0.5 fusion.140
  71.7 0.4 copy-done.6
  72.1 0.5 fusion.139
  72.5 0.3 fusion.17
  72.9 0.3 fusion.19
  73.2 0.2 copy-done.3
  73.4 0.6 fusion.70
  74.0 0.6 fusion.67
  74.6 0.3 copy-done.5
  74.9 0.5 fusion.138
  75.4 0.3 fusion.21
  75.7 0.6 fusion.64
  76.3 0.5 fusion.137
  76.8 0.3 fusion.23
  77.1 0.6 fusion.61
  77.7 0.1 slice-done.1
  77.8 0.6 slice-done.2
  78.4 1.6 multiply_reduce_fusion
  80.0 1.1 copy-done.1
  81.1 1.0 multiply_convert_fusion
  82.1 0.2 reduce-scatter.2.cloned.1.call-start
  82.4 80.9 %all-gather.2.cloned.1.call-done = bf16[2048,2560]{1,0:T(8,128)(2,1)} async-done(((bf16[128,2560]{1,0:T(8,128)(2,1)}), bf16[2048,2560]{1,0:T(8,128)(2,1)}) %all-gather.2.cloned.1.call-update) | async-done | bytes 10485776 | tf_op jit(solution)/shard_map/all_gather | solution.py:99
  163.2 17.2 %fusion = f32[2048,1216]{0,1:T(8,128)S(1)} fusion(bf16[2048,2560]{1,0:T(8,128)(2,1)} %all-gather.2.cloned.1.call-done, bf16[2560,608]{0,1:T(8,128)(2,1)} %param.23, bf16[2560,608]{0,1:T(8,128)(2,1)} %param.22), kind=kOutput, calls=%fused_computation.1 | convolution fusion | flops 12763136000 | bytes 26673152 | tf_op jit(solution)/shard_map/dot_general | solution.py:102
  180.5 11.1 %convolution_convert_fusion = bf16[2048,2560]{1,0:T(8,128)(2,1)} fusion(bf16[608,2560]{1,0:T(8,128)(2,1)S(1)} %copy-done, f32[2048,1216]{0,1:T(8,128)S(1)} %fusion), kind=kOutput, calls=%fused_computation | convolution fusion | flops 6388056064 | bytes 23560192 | tf_op jit(solution)/shard_map/dot_general | solution.py:106
  192.3 89.5 %reduce-scatter.2.cloned.1.call-done = bf16[128,2560]{1,0:T(8,128)(2,1)} async-done(((bf16[2048,2560]{1,0:T(8,128)(2,1)}), bf16[128,2560]{1,0:T(8,128)(2,1)}) %reduce-scatter.2.cloned.1.call-update) | async-done | bytes 655376 | tf_op jit(solution)/shard_map/reduce_scatter | solution.py:107
  281.8 2.5 select_convert_fusion
  (26 shorter events, 0.2 us)
Async XLA Ops:
  6.5 173.9 %copy-start = (bf16[608,2560]{1,0:T(8,128)(2,1)S(1)}, bf16[608,2560]{1,0:T(8,128)(2,1)}, u32[]{:S(2)}) copy-start(bf16[608,2560]{1,0:T(8,128)(2,1)} %param.24) | copy-start | bytes 9338884
  37.8 31.7 %all-to-all-start = ((bf16[8,128,1024]{2,1,0:T(8,128)(2,1)}), bf16[8,128,1024]{2,1,0:T(8,128)(2,1)}, u32[]{:S(2)}, u32[]{:S(2)}) async-start(bf16[8,128,1024]{2,1,0:T(8,128)(2,1)} %fusion.105), calls=%async_computation | async-start | bytes 4194304 | tf_op jit(solution)/shard_map/all_to_all | solution.py:81
  42.2 121.1 %all-gather.2.cloned.1.call-start = ((), (), s32[]{:S(2)}) async-start(), calls=%async_computation.2 | async-start | bytes 11141120 | tf_op jit(solution)/shard_map/all_gather | solution.py:99
  47.2 24.0 %copy-start.2 = (bf16[128,512]{1,0:T(8,128)(2,1)S(1)}, bf16[128,512]{1,0:T(8,128)(2,1)}, u32[]{:S(2)}) copy-start(bf16[128,512]{1,0:T(8,128)(2,1)} %param.16) | copy-start | bytes 393220
  69.5 1.7 copy-start.7
  71.2 0.9 copy-start.6
  72.5 0.9 copy-start.3
  74.0 0.9 copy-start.5
  74.0 3.7 %slice-start = ((s8[10485760]{0:T(1024)(128)(4,1)}), s8[4194304]{0:T(1024)(128)(4,1)S(1)}, s32[]{:S(2)}) async-start(s8[10485760]{0:T(1024)(128)(4,1)} %bitcast.120), calls=%async_computation.4 | async-start | bytes 8388608
  75.4 2.4 slice-start.1
  76.3 2.0 slice-start.2
  77.1 1.2 copy-start.4
  78.4 2.7 copy-start.8
  80.0 1.1 copy-start.1
  82.1 199.7 %reduce-scatter.2.cloned.1.call-start = ((), (), s32[]{:S(2)}) async-start(), calls=%async_computation.3 | async-start | bytes 11141120 | tf_op jit(solution)/shard_map/reduce_scatter | solution.py:107
Sparse Core Ops, SparseCore 0:
  82.2 80.9 all-gather.1
  191.7 89.9 reduce-scatter.1

commit v9 on v4

--- a/solution.py
+++ b/solution.py
@@ -102,7 +102,7 @@
     both_values = jnp.dot(shard_rows, both_weights, preferred_element_type=jnp.float32)
     gate_values = both_values[:, :block_width]
     upward = both_values[:, block_width:]
-    hidden = (jax.nn.silu(gate_values) * upward).astype(jnp.bfloat16)
+    hidden = lax.optimization_barrier((jax.nn.silu(gate_values) * upward).astype(jnp.bfloat16))
     partial_terms = jnp.dot(hidden, down_weight, preferred_element_type=jnp.float32)
     mixed = lax.psum_scatter(
         partial_terms.astype(jnp.bfloat16), "mlp", scatter_dimension=0, tiled=True

time: 266 us -> 267 us (level)
  no operation moved by 1% of the time
where the time goes in v9:
time: 267 us
  waiting for transfers between devices  192 us (72%)
  matrix products  33.9 us (13%)
  between operations  14.3 us (5%)
  local copies, waits for them, and re-layouts  12.1 us (5%)
  other arithmetic  9.52 us (4%)
  starting transfers between devices  4.67 us (2%)
    reduce_scatter x1, waiting for transfers between devices, shards(): lax.psum_scatter(partial_terms.astype(jnp.bfloat16), 'mlp', scatter_dimen...  89.5 us
    all_gather x1, waiting for transfers between devices, shards(): shard_rows = lax.all_gather(normed, 'mlp', axis=0, tiled=True)  80.9 us
    all_to_all x1, waiting for transfers between devices, shards(): lax.all_to_all(send_both, 'req', split_axis=0, concat_axis=0, tiled=True)  22.1 us
    dot_general x1, matrix products, shards(): jnp.dot(shard_rows, both_weights, preferred_element_type=jnp.float32)  17 us
    dot_general x1, matrix products, shards(): jnp.dot(hidden, down_weight, preferred_element_type=jnp.float32)  11.1 us
    unnamed x28, local copies, waits for them, and re-layouts  5.97 us
  transfers between devices with their start and end apart: 3, of which 3 were waited for; matrix products, arithmetic and copies ran while one was open for 2% of the time, Pallas kernels for 0%

profile of v9, /device:TPU:0, one launch (start us, length us, event | category | flops | bytes accessed | tf_op | source)
XLA Modules:
  0.0 266.9 jit_solution(9172621093955936890)
XLA Ops:
  6.5 0.8 compare_select_fusion
  7.3 0.1 reshape.110
  7.4 0.2 dynamic-slice_reduce_fusion
  7.6 0.9 dynamic-slice_reduce_fusion.1
  8.5 0.1 select_reduce_fusion
  8.6 1.4 fusion.115
  10.0 0.6 select_add_fusion.1
  10.6 1.6 pad_maximum_fusion
  12.1 4.4 %all-to-all-start = ((bf16[8,128,1024]{2,1,0:T(8,128)(2,1)}), bf16[8,128,1024]{2,1,0:T(8,128)(2,1)}, u32[]{:S(2)}, u32[]{:S(2)}) async-start(bf16[8,128,1024]{2,1,0:T(8,128)(2,1)} %pad_maximum_fusion), calls=%async_computation | async-start | bytes 4194304 | tf_op jit(solution)/shard_map/all_to_all | solution.py:81
  16.5 0.0 all-gather.2.cloned.1.call-start
  16.6 1.8 fusion.114
  18.4 1.6 copy.71
  20.0 0.7 copy.72
  20.8 0.8 copy.73
  21.5 0.1 copy.74
  21.7 22.1 %all-to-all-done = bf16[8,128,1024]{2,1,0:T(8,128)(2,1)} async-done(((bf16[8,128,1024]{2,1,0:T(8,128)(2,1)}), bf16[8,128,1024]{2,1,0:T(8,128)(2,1)}, u32[]{:S(2)}, u32[]{:S(2)}) %all-to-all-start) | async-done | bytes 2097184 | tf_op jit(solution)/shard_map/all_to_all | solution.py:81
  43.8 1.7 fusion.113
  45.6 0.5 fusion.120
  46.0 0.4 copy-done.6
  46.4 0.5 fusion.119
  46.9 0.3 fusion.15
  47.2 0.3 fusion.17
  47.6 0.2 copy-done.3
  47.8 0.6 fusion.68
  48.4 0.6 fusion.65
  49.0 0.3 copy-done.5
  49.3 0.5 fusion.118
  49.8 0.0 slice-start.1
  49.8 0.3 fusion.19
  50.1 0.6 fusion.62
  50.7 0.0 slice-start.2
  50.7 0.5 fusion.117
  51.2 0.3 fusion.21
  51.5 0.6 fusion.59
  52.1 0.1 slice-done.1
  52.2 0.6 slice-done.2
  52.7 1.6 multiply_reduce_fusion
  54.4 1.1 copy-done.1
  55.5 1.0 multiply_convert_fusion
  56.5 0.0 all-gather.2.cloned.1.call-update
  56.5 0.2 reduce-scatter.2.cloned.1.call-start
  56.7 80.9 %all-gather.2.cloned.1.call-done = bf16[2048,2560]{1,0:T(8,128)(2,1)} async-done(((bf16[128,2560]{1,0:T(8,128)(2,1)}), bf16[2048,2560]{1,0:T(8,128)(2,1)}) %all-gather.2.cloned.1.call-update) | async-done | bytes 10485776 | tf_op jit(solution)/shard_map/all_gather | solution.py:99
  137.6 17.0 %fusion = f32[2048,1216]{0,1:T(8,128)S(1)} fusion(bf16[2048,2560]{1,0:T(8,128)(2,1)} %all-gather.2.cloned.1.call-done, bf16[2560,608]{0,1:T(8,128)(2,1)} %param.23, bf16[2560,608]{0,1:T(8,128)(2,1)} %param.22), kind=kOutput, calls=%fused_computation.1 | convolution fusion | flops 12763136000 | bytes 26673152 | tf_op jit(solution)/shard_map/dot_general | solution.py:102
  154.6 1.6 fusion.4
  156.2 11.1 %convolution_convert_fusion = bf16[2048,2560]{1,0:T(8,128)(2,1)} fusion(bf16[2048,608]{0,1:T(8,128)(2,1)S(1)} %fusion.4, bf16[608,2560]{1,0:T(8,128)(2,1)S(1)} %copy-done), kind=kOutput, calls=%fused_computation | convolution fusion | flops 6380584960 | bytes 16089088 | tf_op jit(solution)/shard_map/dot_general | solution.py:106
  167.4 0.0 reduce-scatter.2.cloned.1.call-update
  168.1 89.5 %reduce-scatter.2.cloned.1.call-done = bf16[128,2560]{1,0:T(8,128)(2,1)} async-done(((bf16[2048,2560]{1,0:T(8,128)(2,1)}), bf16[128,2560]{1,0:T(8,128)(2,1)}) %reduce-scatter.2.cloned.1.call-update) | async-done | bytes 655376 | tf_op jit(solution)/shard_map/reduce_scatter | solution.py:107
  257.6 2.5 select_convert_fusion
  (23 shorter events, 0.1 us)
Async XLA Ops:
  6.5 149.7 %copy-start = (bf16[608,2560]{1,0:T(8,128)(2,1)S(1)}, bf16[608,2560]{1,0:T(8,128)(2,1)}, u32[]{:S(2)}) copy-start(bf16[608,2560]{1,0:T(8,128)(2,1)} %param.24) | copy-start | bytes 9338884
  12.1 31.7 %all-to-all-start = ((bf16[8,128,1024]{2,1,0:T(8,128)(2,1)}), bf16[8,128,1024]{2,1,0:T(8,128)(2,1)}, u32[]{:S(2)}, u32[]{:S(2)}) async-start(bf16[8,128,1024]{2,1,0:T(8,128)(2,1)} %pad_maximum_fusion), calls=%async_computation | async-start | bytes 4194304 | tf_op jit(solution)/shard_map/all_to_all | solution.py:81
  16.5 121.1 %all-gather.2.cloned.1.call-start = ((), (), s32[]{:S(2)}) async-start(), calls=%async_computation.2 | async-start | bytes 11141120 | tf_op jit(solution)/shard_map/all_gather | solution.py:99
  21.5 24.0 %copy-start.2 = (bf16[128,512]{1,0:T(8,128)(2,1)S(1)}, bf16[128,512]{1,0:T(8,128)(2,1)}, u32[]{:S(2)}) copy-start(bf16[128,512]{1,0:T(8,128)(2,1)} %param.16) | copy-start | bytes 393220
  43.8 1.7 copy-start.7
  45.5 0.9 copy-start.6
  46.9 0.9 copy-start.3
  48.4 0.9 copy-start.5
  48.4 3.7 %slice-start = ((s8[10485760]{0:T(1024)(128)(4,1)}), s8[4194304]{0:T(1024)(128)(4,1)S(1)}, s32[]{:S(2)}) async-start(s8[10485760]{0:T(1024)(128)(4,1)} %bitcast.103), calls=%async_computation.4 | async-start | bytes 8388608
  49.8 2.4 slice-start.1
  50.7 2.0 slice-start.2
  51.5 1.2 copy-start.4
  52.7 2.7 %copy-start.8 = (f32[2560]{0:T(1024)S(1)}, f32[2560]{0:T(1024)}, u32[]{:S(2)}) copy-start(f32[2560]{0:T(1024)} %param.21) | copy-start | bytes 30724
  54.4 1.1 copy-start.1
  56.5 201.1 %reduce-scatter.2.cloned.1.call-start = ((), (), s32[]{:S(2)}) async-start(), calls=%async_computation.3 | async-start | bytes 11141120 | tf_op jit(solution)/shard_map/reduce_scatter | solution.py:107
Sparse Core Ops, SparseCore 0:
  56.6 80.9 all-gather.1
  167.5 89.9 reduce-scatter.1
